TPU v7x, 256 devices: a whole 4x4x8 slice. The times are simulated.
256 devices in a mesh: joint: 8 (over z), frame: 32 (over y, x, core).
Axes of the slice: x: 4, y: 4, z: 8, core: 2. Of those that a mesh axis runs over, the one named last changes fastest.
Arguments:
- tokens: bfloat16 [64, 768, 1536], P('joint', 'frame'), may hold values from -500 to 500
- norm_gain: float32 [1536], replicated, may hold values from 0.1 to 1.9
- qkv_weight: bfloat16 [1536, 3072], P('frame'), may hold values from -3 to 3
- out_grad: bfloat16 [64, 768, 1024], P('joint', 'frame'), may hold values from -6 to 6
Outputs:
- attended: bfloat16 [64, 768, 1024], P('joint', 'frame')
- token_grad: bfloat16 [64, 768, 1536], P('joint', 'frame')
- weight_grad: float32 [1536, 3072], P('frame')
- gain_grad: float32 [1536], replicated
All inputs are finite; a program needn't handle non-finite values.
Results may differ from a plain program's by a relative error of at most 0.029.
The roundings to bfloat16 on the way count: a program that leaves them out, or rounds other values in their place, can miss the bound.
Values may be sent and summed in bfloat16 or wider, within the bound.
No kernel may reach another device: no remote copies, remote signals or barrier semaphores. Data moves between devices by JAX's collectives and lax.ppermute only.
A program may use at most 128 MiB of HBM per device.

v0:
```python
import math

import jax
import jax.numpy as jnp
from jax import lax
from jax.sharding import PartitionSpec as P

HEADS = 8
HDIM = 128


EPSILON = 1e-05


def attention_pass(queries, keys_all, values_all, upstream, inv_root):
    scores = (
        jnp.einsum("ifhd,jfhd->fhij", queries, keys_all, preferred_element_type=jnp.float32)
        * inv_root
    )
    probs = jax.nn.softmax(scores, axis=-1)
    probs_low = probs.astype(jnp.bfloat16)
    attended = jnp.einsum(
        "fhij,jfhd->ifhd", probs_low, values_all, preferred_element_type=jnp.float32
    ).astype(jnp.bfloat16)
    prob_grad = jnp.einsum(
        "ifhd,jfhd->fhij", upstream, values_all, preferred_element_type=jnp.float32
    )
    carried = jnp.sum(probs * prob_grad, axis=-1, keepdims=True)
    score_grad = (probs * (prob_grad - carried) * inv_root).astype(jnp.bfloat16)
    query_grad = jnp.einsum(
        "fhij,jfhd->ifhd", score_grad, keys_all, preferred_element_type=jnp.float32
    ).astype(jnp.bfloat16)
    return (attended, probs_low, score_grad, query_grad)


def per_device(tokens, norm_gain, qkv_weight, out_grad):
    joint_rows, frame_rows, width = tokens.shape
    inner = out_grad.shape[2]
    count = joint_rows * frame_rows
    joint_count = lax.axis_size("joint")
    total_tokens = count * joint_count * lax.axis_size("frame")
    grad_scale = 1.0 / math.sqrt(total_tokens)
    inv_root = 1.0 / math.sqrt(HDIM)
    flat = tokens.reshape(count, width).astype(jnp.float32)
    rinv = lax.rsqrt(jnp.mean(flat * flat, axis=1, keepdims=True) + EPSILON)
    normed = flat * rinv
    scaled = (normed * norm_gain).astype(jnp.bfloat16)
    whole = lax.all_gather(qkv_weight, "frame", axis=0, tiled=True)
    projected = jnp.dot(scaled, whole, preferred_element_type=jnp.float32)
    projected = projected.astype(jnp.bfloat16).reshape(joint_rows, frame_rows, 3 * inner)
    queries = projected[:, :, :inner].reshape(joint_rows, frame_rows, HEADS, HDIM)
    keyvals = lax.all_gather(projected[:, :, inner:], "joint", axis=0, tiled=True)
    joints = keyvals.shape[0]
    keyvals = keyvals.reshape(joints, frame_rows, 2, HEADS, HDIM)
    keys_all = keyvals[:, :, 0]
    values_all = keyvals[:, :, 1]
    upstream = out_grad.reshape(joint_rows, frame_rows, HEADS, HDIM)
    attended, probs_low, score_grad, query_grad = attention_pass(
        queries, keys_all, values_all, upstream, inv_root
    )
    attended = attended.reshape(joint_rows, frame_rows, inner)
    key_part = jnp.einsum(
        "fhij,ifhd->jfhd", score_grad, queries, preferred_element_type=jnp.float32
    )
    value_part = jnp.einsum(
        "fhij,ifhd->jfhd", probs_low, upstream, preferred_element_type=jnp.float32
    )
    both_parts = jnp.stack([key_part, value_part], axis=2).reshape(joints, frame_rows, 2 * inner)
    kv_grad = lax.psum_scatter(
        both_parts.astype(jnp.bfloat16), "joint", scatter_dimension=0, tiled=True
    )
    qkv_grad = jnp.concatenate(
        [query_grad.reshape(joint_rows, frame_rows, inner), kv_grad], axis=2
    ).reshape(count, 3 * inner)
    product = lax.dot_general(
        scaled, qkv_grad, (((0,), (0,)), ((), ())), preferred_element_type=jnp.float32
    )
    frame_sum = lax.psum_scatter(
        (product * grad_scale).astype(jnp.bfloat16), "frame", scatter_dimension=0, tiled=True
    )
    normed_grad = lax.dot_general(
        qkv_grad, whole, (((1,), (1,)), ((), ())), preferred_element_type=jnp.float32
    )
    gain_part = jnp.sum(normed_grad * normed, axis=0) * grad_scale
    weight_grad = lax.psum(frame_sum, "joint").astype(jnp.float32)
    gain_grad = lax.psum(gain_part, ("joint", "frame"))
    upper = normed_grad * norm_gain
    token_grad = rinv * (upper - normed * jnp.mean(upper * normed, axis=1, keepdims=True))
    token_grad = token_grad.astype(jnp.bfloat16).reshape(joint_rows, frame_rows, width)
    return (attended, token_grad, weight_grad, gain_grad)


def solution(mesh):
    placed = (P("joint", "frame", None), P(), P("frame", None), P("joint", "frame", None))
    return jax.shard_map(
        per_device,
        mesh=mesh,
        in_specs=placed,
        out_specs=(P("joint", "frame", None), P("joint", "frame", None), P("frame", None), P()),
        check_vma=False,
    )
```

profile of v0, /device:TPU:2, one launch (start us, length us, event | category | flops | bytes accessed | tf_op | source)
XLA Modules:
  0.0 475.8 jit_solution(3397268543236490)
XLA Ops:
  7.2 0.0 copy-start.7
  7.2 0.0 all-gather.3.cloned.1.call-start
  7.2 0.7 all-gather.3.cloned.1.call-update
  7.9 0.0 all-gather.5.cloned.1.call-start
  8.0 1.2 multiply_reduce_fusion.2
  9.2 0.1 rsqrt.12
  9.3 1.2 bitcast_multiply_fusion
  10.5 0.0 copy-start.3
  10.5 63.2 %all-gather.3.cloned.1.call-done = bf16[1536,3072]{1,0:T(8,128)(2,1)} async-done(((bf16[48,3072]{1,0:T(8,128)(2,1)}), bf16[1536,3072]{1,0:T(8,128)(2,1)}) %all-gather.3.cloned.1.call-update) | async-done | bytes 9437200 | tf_op jit(solution)/shard_map/all_gather | solution.py:48
  73.7 0.0 copy-done.7
  73.7 5.7 %convolution_convert_fusion = bf16[192,3072]{1,0:T(8,128)(2,1)S(1)} fusion(bf16[1536,3072]{1,0:T(8,128)(2,1)} %all-gather.3.cloned.1.call-done, f32[192,1536]{1,0:T(8,128)S(1)} %bitcast_multiply_fusion, f32[1536]{0:T(1024)S(1)} %copy-done.7), kind=kOutput, calls=%fused_computation.4 | convolution fusion | flops 1813118976 | bytes 11802624 | tf_op jit(solution)/shard_map/dot_general | solution.py:49
  79.4 0.0 copy-done.3
  79.4 0.0 copy-start.5
  79.4 1.0 slice.16
  80.4 0.0 all-gather.5.cloned.1.call-update
  80.4 0.2 reduce-scatter.3.cloned.1.call-start
  80.7 0.0 copy-done.5
  80.7 0.1 copy.32
  80.8 0.8 copy.31
  81.6 73.0 %all-gather.5.cloned.1.call-done = bf16[64,24,2048]{2,1,0:T(8,128)(2,1)} async-done(((bf16[8,24,2048]{2,1,0:T(8,128)(2,1)}), bf16[64,24,2048]{2,1,0:T(8,128)(2,1)}) %all-gather.5.cloned.1.call-update) | async-done | bytes 6291472 | tf_op jit(solution)/shard_map/all_gather | solution.py:52
  154.7 5.1 %copy.30 = bf16[192,8,16,128]{3,2,1,0:T(8,128)(2,1)S(1)} copy(bf16[192,8,16,128]{3,1,2,0:T(8,128)(2,1)} %bitcast.69) | data formatting | bytes 12582912
  159.8 1.8 fusion.37
  161.6 0.0 copy-start.1
  161.6 3.1 fusion.7
  164.8 0.0 copy-done.1
  164.8 5.4 %fusion.38 = (f32[24,8,8]{2,1,0:T(8,128)}, f32[24,8,8,64]{3,2,1,0:T(8,128)}) fusion(bf16[64,24,1,8,128]{4,3,2,1,0:T(8,128)(2,1)S(1)} %get-tuple-element.6, bf16[8,24,8,128]{3,2,1,0:T(8,128)(2,1)} %bitcast.72), kind=kOutput, calls=%fused_computation.56 | convolution fusion | flops 25460800 | bytes 3938304 | tf_op jit(solution)/shard_map/sub | solution.py:20
  170.1 4.8 %convert_bitcast_fusion = bf16[64,24,1,8,128]{4,0,3,1,2:T(8,128)(2,1)} fusion(bf16[8,24,8,128]{3,2,1,0:T(8,128)(2,1)S(1)} %bitcast.71, f32[24,8,8,64]{3,2,1,0:T(8,128)} %get-tuple-element.9, f32[24,8,8]{2,1,0:T(8,128)} %get-tuple-element.8), kind=kOutput, calls=%fused_computation.7 | convolution fusion | flops 26935296 | bytes 3938304 | tf_op jit(solution)/shard_map/fhij,ifhd->jfhd/dot_general | solution.py:65
  175.0 13.5 %convert_bitcast_fusion.1 = bf16[64,24,1,8,128]{4,0,3,1,2:T(8,128)(2,1)} fusion(f32[24,8,8,64]{3,2,1,0:T(8,128)} %fusion.7, bf16[8,24,8,128]{3,2,1,0:T(8,128)(2,1)} %bitcast.73, f32[24,8,8,64]{3,2,1,0:T(8,128)} %get-tuple-element.9, f32[24,8,8]{2,1,0:T(8,128)} %get-tuple-element.8), kind=kOutput, calls=%fused_computation.8 | convolution fusion | flops 27428416 | bytes 4331520 | tf_op jit(solution)/shard_map/fhij,ifhd->jfhd/dot_general | solution.py:62
  188.5 3.4 pad_maximum_fusion
  192.0 6.7 %copy.27 = bf16[64,24,2,8,128]{4,3,2,1,0:T(8,128)(2,1)} copy(bf16[64,24,2,8,128]{4,0,3,1,2:T(8,128)(2,1)S(1)} %pad_maximum_fusion) | data formatting | bytes 12582912 | tf_op jit(solution)/shard_map/stack | solution.py:68
  198.6 10.3 %convert_element_type.57 = bf16[64,24,2048]{2,1,0:T(8,128)(2,1)} reshape(bf16[64,24,2,8,128]{4,3,2,1,0:T(8,128)(2,1)} %copy.27) | data formatting | bytes 12582912 | tf_op jit(solution)/shard_map/convert_element_type | solution.py:70
  208.9 0.0 reduce-scatter.3.cloned.1.call-update
  209.0 0.0 reduce-scatter.5.cloned.1.call-start
  209.0 10.1 %fusion.17 = bf16[8,24,8,128]{3,0,2,1:T(8,128)(2,1)S(1)} fusion(bf16[64,24,1,8,128]{4,3,2,1,0:T(8,128)(2,1)S(1)} %get-tuple-element.6, f32[24,8,8,64]{3,2,1,0:T(8,128)} %fusion.7, f32[24,8,8,64]{3,2,1,0:T(8,128)} %get-tuple-element.9, f32[24,8,8]{2,1,0:T(8,128)} %get-tuple-element.8), kind=kOutput, calls=%fused_computation.24 | convolution fusion | flops 26052160 | bytes 4331520 | tf_op jit(solution)/shard_map/fhij,jfhd->ifhd/dot_general | solution.py:30
  219.2 0.1 copy.24
  219.2 0.1 copy.65
  219.3 63.6 %reduce-scatter.3.cloned.1.call-done = bf16[8,24,2048]{2,1,0:T(8,128)(2,1)} async-done(((bf16[64,24,2048]{2,1,0:T(8,128)(2,1)}), bf16[8,24,2048]{2,1,0:T(8,128)(2,1)}) %reduce-scatter.3.cloned.1.call-update) | async-done | bytes 786448 | tf_op jit(solution)/shard_map/reduce_scatter | solution.py:69
  282.9 7.8 %multiply_convert_fusion = bf16[1536,3072]{1,0:T(8,128)(2,1)} fusion(bf16[192,2048]{1,0:T(8,128)(2,1)} %bitcast.82, bf16[192,1024]{1,0:T(8,128)(2,1)S(1)} %bitcast.80, f32[192,1536]{1,0:T(8,128)} %copy-done.3, f32[1536]{0:T(1024)S(1)} %copy-done.7), kind=kOutput, calls=%fused_computation.2 | convolution fusion | flops 1824325632 | bytes 11802624 | tf_op jit(solution)/shard_map/dot_general | solution.py:75
  290.7 0.0 copy-start.2
  290.7 0.0 copy-start.6
  290.7 0.0 reduce-scatter.5.cloned.1.call-update
  290.7 0.0 copy-start
  290.7 0.0 copy-start.4
  290.7 0.3 all-reduce.2.cloned.1.call-start
  291.0 0.8 copy-done.2
  291.8 0.0 copy-done.6
  291.8 4.1 fusion.16
  295.9 0.1 copy.22
  296.0 0.9 reshape.64
  296.9 0.0 copy-done
  296.9 0.0 copy-done.4
  296.9 8.5 %multiply_reduce_fusion = (f32[1536]{0:T(1024)S(1)}, f32[192]{0:T(256)S(1)}, f32[192,1536]{1,0:T(8,128)}) fusion(f32[192]{0:T(256)S(1)} %rsqrt.12, bf16[8,24,1536]{2,1,0:T(8,128)(2,1)S(1)} %copy-done, f32[192,1536]{1,0:T(8,128)S(1)} %copy-done.4, f32[1536]{0:T(1024)S(1)} %copy-done.7, bf16[1536,3072]{1,0:T(8,128)(2,1)} %all-gather.3.cloned.1.call-done, ...), kind=kOutput, calls=%fused_computation.27 | convolution fusion | flops 1816361216 | bytes 13579776 | tf_op jit(solution)/shard_map/dot_general | solution.py:81
  305.4 74.5 %psum.15 = f32[1536]{0:T(1024)} all-reduce(f32[1536]{0:T(1024)S(1)} %broadcast_multiply_fusion), channel_id=1, replica_groups=mesh['joint'=8,'frame'=32] {'joint','frame'}, use_global_device_ids=true, to_apply=%region_9.0 | all-reduce | flops 1536 | bytes 12288 | tf_op jit(solution)/shard_map/psum | solution.py:86
  379.9 12.5 %reduce-scatter.5.cloned.1.call-done = bf16[48,3072]{1,0:T(8,128)(2,1)} async-done(((bf16[1536,3072]{1,0:T(8,128)(2,1)}), bf16[48,3072]{1,0:T(8,128)(2,1)}) %reduce-scatter.5.cloned.1.call-update) | async-done | bytes 294928 | tf_op jit(solution)/shard_map/reduce_scatter | solution.py:78
  392.4 0.0 all-reduce.2.cloned.1.call-update
  392.4 2.4 multiply_convert_fusion.1
  394.8 72.6 %all-reduce.2.cloned.1.call-done = bf16[48,3072]{1,0:T(8,128)(2,1)} async-done(((bf16[48,3072]{1,0:T(8,128)(2,1)}), bf16[48,3072]{1,0:T(8,128)(2,1)}) %all-reduce.2.cloned.1.call-update) | async-done | bytes 294928 | tf_op jit(solution)/shard_map/psum | solution.py:85
  467.4 1.8 convert_element_type.60
  (4 shorter events, 0.0 us)
Async XLA Ops:
  7.2 66.6 %copy-start.7 = (f32[1536]{0:T(1024)S(1)}, f32[1536]{0:T(1024)}, u32[]{:S(2)}) copy-start(f32[1536]{0:T(1024)} %param.5) | copy-start | bytes 18436
  7.2 66.6 %all-gather.3.cloned.1.call-start = ((), (), s32[]{:S(2)}) async-start(), calls=%async_computation.2 | async-start | bytes 9732096 | tf_op jit(solution)/shard_map/all_gather | solution.py:48
  7.9 146.7 %all-gather.5.cloned.1.call-start = ((), (), s32[]{:S(2)}) async-start(), calls=%async_computation.3 | async-start | bytes 7077888 | tf_op jit(solution)/shard_map/all_gather | solution.py:52
  10.5 68.9 %copy-start.3 = (f32[192,1536]{1,0:T(8,128)}, f32[192,1536]{1,0:T(8,128)S(1)}, u32[]{:S(2)}) copy-start(f32[192,1536]{1,0:T(8,128)S(1)} %bitcast_multiply_fusion) | copy-start | bytes 3538948
  79.4 1.2 copy-start.5
  80.4 202.4 %reduce-scatter.3.cloned.1.call-start = ((), (), s32[]{:S(2)}) async-start(), calls=%async_computation.4 | async-start | bytes 7077888 | tf_op jit(solution)/shard_map/reduce_scatter | solution.py:69
  161.6 3.1 copy-start.1
  209.0 183.4 %reduce-scatter.5.cloned.1.call-start = ((), (), s32[]{:S(2)}) async-start(), calls=%async_computation.5 | async-start | bytes 9732096 | tf_op jit(solution)/shard_map/reduce_scatter | solution.py:78
  290.7 1.1 copy-start.2
  290.7 1.1 copy-start.6
  290.7 6.2 %copy-start = (bf16[8,24,1536]{2,1,0:T(8,128)(2,1)S(1)}, bf16[8,24,1536]{2,1,0:T(8,128)(2,1)}, u32[]{:S(2)}) copy-start(bf16[8,24,1536]{2,1,0:T(8,128)(2,1)} %param.4) | copy-start | bytes 1769476
  290.7 6.2 %copy-start.4 = (f32[192,1536]{1,0:T(8,128)S(1)}, f32[192,1536]{1,0:T(8,128)}, u32[]{:S(2)}) copy-start(f32[192,1536]{1,0:T(8,128)} %copy-done.3) | copy-start | bytes 3538948
  290.7 176.7 %all-reduce.2.cloned.1.call-start = ((), (), s32[]{:S(2)}) async-start(), calls=%async_computation.6 | async-start | bytes 589824 | tf_op jit(solution)/shard_map/psum | solution.py:85
Sparse Core Ops, SparseCore 0:
  10.5 63.1 all-gather.2
  80.6 74.0 all-gather.4
  209.1 73.7 reduce-scatter.2
  290.8 101.5 reduce-scatter.4
  394.6 72.7 all-reduce.1
where the time goes:
time: 477 us; the launch traced here: 476 us
  waiting for transfers between devices  286 us (60%)
  blocking collectives  74.5 us (16%)
  matrix products  63.1 us (13%)
  local copies, waits for them, and re-layouts  27.8 us (6%)
  between operations  13.9 us (3%)
  other arithmetic  10.1 us (2%)
    psum x1, blocking collectives, per_device(): gain_grad = lax.psum(gain_part, ('joint', 'frame'))  74.5 us
    all_gather x1, waiting for transfers between devices, per_device(): lax.all_gather(projected[:, :, inner:], 'joint', axis=0, tiled=True)  73 us
    psum x1, waiting for transfers between devices, per_device(): weight_grad = lax.psum(frame_sum, 'joint').astype(jnp.float32)  72.6 us
    reduce_scatter x1, waiting for transfers between devices, per_device(): lax.psum_scatter(both_parts.astype(jnp.bfloat16), 'joint', scatter_dimens...  63.6 us
    all_gather x1, waiting for transfers between devices, per_device(): whole = lax.all_gather(qkv_weight, 'frame', axis=0, tiled=True)  63.2 us
    dot_general x1, matrix products, per_device(): jnp.einsum('fhij,ifhd->jfhd', score_grad, queries, preferred_element_type...  13.5 us
    reduce_scatter x1, waiting for transfers between devices, per_device(): lax.psum_scatter((product * grad_scale).astype(jnp.bfloat16), 'frame', sc...  12.5 us
    convert_element_type x1, local copies, waits for them, and re-layouts, per_device(): both_parts.astype(jnp.bfloat16)  10.3 us
  transfers between devices with their start and end apart: 5, of which 5 were waited for; matrix products, arithmetic and copies ran while one was open for 6% of the time, Pallas kernels for 0%

commit v1 on v0

v1 whole, which is shorter than its diff:
```python
import math

import jax
import jax.numpy as jnp
from jax import lax
from jax.sharding import PartitionSpec as P

HEADS = 8
HDIM = 128


EPSILON = 1e-05


def attention_local(queries, keys_all, values_all, upstream, inv_root, groups):
    scores = (
        jnp.einsum("fihd,fjhd->fhij", queries, keys_all, preferred_element_type=jnp.float32)
        * inv_root
    )
    probs = jax.nn.softmax(scores, axis=-1)
    probs_low = probs.astype(jnp.bfloat16)
    attended = jnp.einsum(
        "fhij,fjhd->fihd", probs_low, values_all, preferred_element_type=jnp.float32
    ).astype(jnp.bfloat16)
    prob_grad = jnp.einsum(
        "fihd,fjhd->fhij", upstream, values_all, preferred_element_type=jnp.float32
    )
    carried = jnp.sum(probs * prob_grad, axis=-1, keepdims=True)
    score_grad = (probs * (prob_grad - carried) * inv_root).astype(jnp.bfloat16)
    query_grad = jnp.einsum(
        "fhij,fjhd->fihd", score_grad, keys_all, preferred_element_type=jnp.float32
    ).astype(jnp.bfloat16)
    frames, joints = queries.shape[0], queries.shape[1]
    size = joints // groups
    sg = score_grad.reshape(frames, HEADS, groups, size, joints)
    pl_ = probs_low.reshape(frames, HEADS, groups, size, joints)
    qg = queries.reshape(frames, groups, size, HEADS, HDIM)
    ug = upstream.reshape(frames, groups, size, HEADS, HDIM)
    key_part = jnp.einsum("fhgij,fgihd->fgjhd", sg, qg, preferred_element_type=jnp.float32)
    value_part = jnp.einsum("fhgij,fgihd->fgjhd", pl_, ug, preferred_element_type=jnp.float32)
    key_grad = jnp.sum(key_part.astype(jnp.bfloat16).astype(jnp.float32), axis=1).astype(jnp.bfloat16)
    value_grad = jnp.sum(value_part.astype(jnp.bfloat16).astype(jnp.float32), axis=1).astype(
        jnp.bfloat16
    )
    return attended, query_grad, key_grad, value_grad


def per_device(tokens, norm_gain, qkv_weight, out_grad):
    joint_rows, frame_rows, width = tokens.shape
    inner = out_grad.shape[2]
    joint_count = lax.axis_size("joint")
    total_tokens = joint_rows * frame_rows * joint_count * lax.axis_size("frame")
    grad_scale = 1.0 / math.sqrt(total_tokens)
    inv_root = 1.0 / math.sqrt(HDIM)
    joints = joint_rows * joint_count
    local_frames = frame_rows // joint_count
    count = joints * local_frames

    whole = lax.all_gather(qkv_weight, "frame", axis=0, tiled=True)

    packed = jnp.concatenate([tokens, out_grad], axis=2)
    packed = lax.all_to_all(packed, "joint", 1, 0, tiled=True)
    packed = packed.transpose(1, 0, 2)
    flat = packed[:, :, :width].reshape(count, width).astype(jnp.float32)
    upstream = packed[:, :, width:].reshape(local_frames, joints, HEADS, HDIM)

    rinv = lax.rsqrt(jnp.mean(flat * flat, axis=1, keepdims=True) + EPSILON)
    normed = flat * rinv
    scaled = (normed * norm_gain).astype(jnp.bfloat16)
    projected = jnp.dot(scaled, whole, preferred_element_type=jnp.float32).astype(jnp.bfloat16)
    projected = projected.reshape(local_frames, joints, 3, HEADS, HDIM)
    queries = projected[:, :, 0]
    keys_all = projected[:, :, 1]
    values_all = projected[:, :, 2]
    attended, query_grad, key_grad, value_grad = attention_local(
        queries, keys_all, values_all, upstream, inv_root, joint_count
    )
    qkv_grad = jnp.concatenate(
        [
            query_grad.reshape(count, inner),
            key_grad.reshape(count, inner),
            value_grad.reshape(count, inner),
        ],
        axis=1,
    )
    product = lax.dot_general(
        scaled, qkv_grad, (((0,), (0,)), ((), ())), preferred_element_type=jnp.float32
    )
    frame_sum = lax.psum_scatter(
        (product * grad_scale).astype(jnp.bfloat16), "frame", scatter_dimension=0, tiled=True
    )
    joint_part = lax.psum_scatter(frame_sum, "joint", scatter_dimension=1, tiled=True)
    weight_grad = lax.all_gather(joint_part, "joint", axis=1, tiled=True).astype(jnp.float32)
    normed_grad = lax.dot_general(
        qkv_grad, whole, (((1,), (1,)), ((), ())), preferred_element_type=jnp.float32
    )
    gain_part = jnp.sum(normed_grad * normed, axis=0) * grad_scale
    gain_grad = lax.psum(gain_part, ("joint", "frame"))
    upper = normed_grad * norm_gain
    token_grad = rinv * (upper - normed * jnp.mean(upper * normed, axis=1, keepdims=True))
    token_grad = token_grad.astype(jnp.bfloat16).reshape(local_frames, joints, width)
    back = jnp.concatenate(
        [attended.reshape(local_frames, joints, inner), token_grad], axis=2
    ).transpose(1, 0, 2)
    back = lax.all_to_all(back, "joint", 0, 1, tiled=True)
    attended_out = back[:, :, :inner]
    token_out = back[:, :, inner:]
    return (attended_out, token_out, weight_grad, gain_grad)


def solution(mesh):
    placed = (P("joint", "frame", None), P(), P("frame", None), P("joint", "frame", None))
    return jax.shard_map(
        per_device,
        mesh=mesh,
        in_specs=placed,
        out_specs=(P("joint", "frame", None), P("joint", "frame", None), P("frame", None), P()),
        check_vma=False,
    )
```

time: 477 us -> 319 us (0.67)
  waiting for transfers between devices: 286 us -> 113 us
  blocking collectives: 74.5 us -> 134 us
  matrix products: 63.1 us -> 28.2 us
  local copies, waits for them, and re-layouts: 27.8 us -> 14.4 us
  starting transfers between devices: 0.64 us -> 7.13 us
    all_gather x1 -> x0, waiting for transfers between devices: 73 us -> none  [per_device(): lax.all_gather(projected[:, :, inner:], 'joint', axis=0, tiled=True)]
    psum x1 -> x0, waiting for transfers between devices: 72.6 us -> none  [per_device(): weight_grad = lax.psum(frame_sum, 'joint').astype(jnp.float32)]
    reduce_scatter x1, waiting for transfers between devices: 12.5 us -> 84.1 us  [per_device(): lax.psum_scatter((product * grad_scale).astype(jnp.bfloat16), 'frame', sc...]
    reduce_scatter x1 -> x0, waiting for transfers between devices: 63.6 us -> none  [per_device(): lax.psum_scatter(both_parts.astype(jnp.bfloat16), 'joint', scatter_dimens...]
    all_to_all x0 -> x1, blocking collectives: none -> 35.6 us  [per_device(): packed = lax.all_to_all(packed, 'joint', 1, 0, tiled=True)]
    all_gather x1, waiting for transfers between devices: 63.2 us -> 27.9 us  [per_device(): whole = lax.all_gather(qkv_weight, 'frame', axis=0, tiled=True)]
    dot_general x6, matrix products: 41.4 us -> 13.2 us  [the longest x1 5.69 us: per_device(): jnp.dot(scaled, whole, preferred_element_type=jnp.float32)]
    all_gather x0 -> x1, blocking collectives: none -> 25.1 us  [per_device(): lax.all_gather(joint_part, 'joint', axis=1, tiled=True).astype(jnp.float32)]
  transfers between devices with their start and end apart: 5 -> 4, of which waited for: 5 -> 2; matrix products, arithmetic and copies ran while one was open for 6% -> 5% of each run, Pallas kernels for 0% -> 0%
where the time goes in v1:
time: 319 us; the launch traced here: 317 us
  blocking collectives  134 us (42%)
  waiting for transfers between devices  113 us (35%)
  matrix products  28.2 us (9%)
  local copies, waits for them, and re-layouts  14.4 us (5%)
  between operations  14.1 us (4%)
  starting transfers between devices  7.13 us (2%)
  other arithmetic  5.87 us (2%)
    reduce_scatter x1, waiting for transfers between devices, per_device(): lax.psum_scatter((product * grad_scale).astype(jnp.bfloat16), 'frame', sc...  84.1 us
    psum x1, blocking collectives, per_device(): gain_grad = lax.psum(gain_part, ('joint', 'frame'))  73.7 us
    all_to_all x1, blocking collectives, per_device(): packed = lax.all_to_all(packed, 'joint', 1, 0, tiled=True)  35.6 us
    all_gather x1, waiting for transfers between devices, per_device(): whole = lax.all_gather(qkv_weight, 'frame', axis=0, tiled=True)  27.9 us
    all_gather x1, blocking collectives, per_device(): lax.all_gather(joint_part, 'joint', axis=1, tiled=True).astype(jnp.float32)  25.1 us
    unnamed x29, local copies, waits for them, and re-layouts  9.18 us
    dot_general x1, matrix products, per_device(): lax.dot_general(qkv_grad, whole, (((1,), (1,)), ((), ())), preferred_elem...  7.44 us
    all_to_all x1, starting transfers between devices, per_device(): back = lax.all_to_all(back, 'joint', 0, 1, tiled=True)  7.01 us
  transfers between devices with their start and end apart: 4, of which 2 were waited for; matrix products, arithmetic and copies ran while one was open for 5% of the time, Pallas kernels for 0%

profile of v1, /device:TPU:2, one launch (start us, length us, event | category | flops | bytes accessed | tf_op | source)
XLA Modules:
  0.0 316.7 jit_solution(16296569881700968422)
XLA Ops:
  7.2 0.0 all-gather.2.cloned.1.call-start
  7.2 0.7 all-gather.2.cloned.1.call-update
  7.9 0.0 reduce-scatter.5.cloned.1.call-start
  8.0 1.2 copy.77
  9.2 0.2 copy.76
  9.4 0.1 pad_maximum_fusion
  9.4 35.6 %all_to_all.36 = bf16[8,24,2560]{2,0,1:T(8,128)(2,1)S(1)} all-to-all(bf16[8,24,2560]{2,0,1:T(8,128)(2,1)S(1)} %pad_maximum_fusion), channel_id=1, replica_groups=mesh['joint'=8,'frame'=32] {'joint'}, dimensions={1} | all-to-all | bytes 1966080 | tf_op jit(solution)/shard_map/all_to_all | solution.py:62
  45.0 0.1 copy.151
  45.1 0.2 multiply_reduce_fusion.2
  45.3 0.1 rsqrt.12
  45.4 0.1 slice_convert_fusion
  45.5 0.0 copy-start.9
  45.6 0.1 bitcast_multiply_fusion
  45.7 27.9 %all-gather.2.cloned.1.call-done = bf16[1536,3072]{1,0:T(8,128)(2,1)} async-done(((bf16[48,3072]{1,0:T(8,128)(2,1)}), bf16[1536,3072]{1,0:T(8,128)(2,1)}) %all-gather.2.cloned.1.call-update) | async-done | bytes 9437200 | tf_op jit(solution)/shard_map/all_gather | solution.py:59
  73.6 5.7 %fusion.3 = bf16[24,8,24,128]{3,1,2,0:T(8,128)(2,1)S(1)} fusion(bf16[1536,3072]{1,0:T(8,128)(2,1)} %all-gather.2.cloned.1.call-done, f32[192,1536]{1,0:T(8,128)S(1)} %bitcast_multiply_fusion, f32[1536]{0:T(1024)S(1)} %copy-done.9), kind=kOutput, calls=%fused_computation.7 | convolution fusion | flops 1813118976 | bytes 11802624 | tf_op jit(solution)/shard_map/dot_general | solution.py:70
  79.3 0.0 copy-done
  79.4 0.2 copy.111
  79.6 1.1 fusion.27
  80.7 0.3 fusion.12
  81.0 2.4 fusion.28
  83.4 2.7 fusion.10
  86.1 2.4 fusion.8
  88.5 0.0 copy-done.3
  88.5 0.1 fusion.26
  88.6 0.9 copy.91
  89.6 2.1 convert_reduce_fusion
  91.7 0.0 copy-start.5
  91.7 0.3 copy.93
  92.0 0.0 copy-done.7
  92.0 0.9 copy.87
  92.9 2.1 convert_reduce_fusion.1
  95.0 0.3 copy.90
  95.3 0.0 copy-done.6
  95.3 0.3 copy.86
  95.6 0.0 copy-start.1
  95.6 0.1 bitcast_dynamic-update-slice_fusion.2
  95.6 0.1 bitcast_dynamic-update-slice_fusion.1
  95.7 0.1 bitcast_dynamic-update-slice_fusion
  95.8 1.0 copy-done.8
  96.8 0.4 copy-done.1
  97.2 5.1 %multiply_convert_fusion = bf16[1536,3072]{1,0:T(8,128)(2,1)} fusion(bf16[192,3072]{1,0:T(8,128)(2,1)S(1)} %bitcast_dynamic-update-slice_fusion, f32[192,1536]{1,0:T(8,128)S(1)} %copy-done.1, f32[1536]{0:T(1024)S(1)} %copy-done.9), kind=kOutput, calls=%fused_computation.2 | convolution fusion | flops 1821966336 | bytes 11802624 | tf_op jit(solution)/shard_map/dot_general | solution.py:86
  102.3 0.0 reduce-scatter.5.cloned.1.call-update
  102.3 0.3 fusion.9
  102.6 0.3 copy.102
  102.9 0.1 reshape.73
  103.0 0.9 copy-done.2
  103.9 7.4 %multiply_reduce_fusion = (f32[1536]{0:T(1024)S(1)}, f32[192]{0:T(256)S(1)}, f32[192,1536]{1,0:T(8,128)S(1)}) fusion(f32[192,1536]{1,0:T(8,128)S(1)} %copy-done.2, f32[1536]{0:T(1024)S(1)} %copy-done.9, bf16[192,3072]{1,0:T(8,128)(2,1)} %copy-done.8, bf16[1536,3072]{1,0:T(8,128)(2,1)} %all-gather.2.cloned.1.call-done), kind=kOutput, calls=%fused_computation.20 | convolution fusion | flops 1813412096 | bytes 12989184 | tf_op jit(solution)/shard_map/dot_general | solution.py:94
  111.4 0.3 multiply_convert_fusion.1
  111.7 0.5 copy.95
  112.2 1.7 maximum_bitcast_fusion
  113.8 7.0 %all-to-all-start.1 = ((bf16[64,3,2560]{2,1,0:T(4,128)(2,1)}), bf16[64,3,2560]{2,1,0:T(4,128)(2,1)S(1)}, u32[]{:S(2)}, u32[]{:S(2)}) async-start(bf16[64,3,2560]{2,1,0:T(4,128)(2,1)} %maximum_bitcast_fusion), calls=%async_computation.1 | async-start | bytes 2621440 | tf_op jit(solution)/shard_map/all_to_all | solution.py:105
  120.8 0.0 reduce-scatter.7.cloned.1.call-start
  120.9 84.1 %reduce-scatter.5.cloned.1.call-done = bf16[48,3072]{1,0:T(8,128)(2,1)} async-done(((bf16[1536,3072]{1,0:T(8,128)(2,1)}), bf16[48,3072]{1,0:T(8,128)(2,1)}) %reduce-scatter.5.cloned.1.call-update) | async-done | bytes 294928 | tf_op jit(solution)/shard_map/reduce_scatter | solution.py:89
  204.9 2.2 copy.103
  207.1 0.0 reduce-scatter.7.cloned.1.call-update
  207.1 73.7 %psum.7 = f32[1536]{0:T(1024)} all-reduce(f32[1536]{0:T(1024)S(1)} %broadcast_multiply_fusion), channel_id=1, replica_groups=mesh['joint'=8,'frame'=32] {'joint','frame'}, use_global_device_ids=true, to_apply=%region_10.0 | all-reduce | flops 1536 | bytes 12288 | tf_op jit(solution)/shard_map/psum | solution.py:98
  280.8 0.0 all-to-all-done.1
  280.8 0.2 copy.150
  281.0 0.1 copy.97
  281.2 1.0 copy.99
  282.2 1.0 copy.98
  283.2 1.0 copy.104
  284.2 25.1 %all_gather.7 = bf16[48,3072]{1,0:T(8,128)(2,1)S(1)} all-gather(bf16[48,384]{1,0:T(8,128)(2,1)S(1)} %copy.104), channel_id=1, replica_groups=mesh['joint'=8,'frame'=32] {'joint'}, dimensions={1}, use_global_device_ids=true | all-gather | bytes 331776 | tf_op jit(solution)/shard_map/all_gather | solution.py:93
  309.3 0.9 convert_element_type.69
  (16 shorter events, 0.1 us)
Async XLA Ops:
  7.2 2.0 copy-start.4
  7.2 66.5 %all-gather.2.cloned.1.call-start = ((), (), s32[]{:S(2)}) async-start(), calls=%async_computation.4 | async-start | bytes 9732096 | tf_op jit(solution)/shard_map/all_gather | solution.py:59
  7.9 197.0 %reduce-scatter.5.cloned.1.call-start = ((), (), s32[]{:S(2)}) async-start(), calls=%async_computation.5 | async-start | bytes 9732096 | tf_op jit(solution)/shard_map/reduce_scatter | solution.py:89
  45.5 28.1 %copy-start.9 = (f32[1536]{0:T(1024)S(1)}, f32[1536]{0:T(1024)}, u32[]{:S(2)}) copy-start(f32[1536]{0:T(1024)} %param.5) | copy-start | bytes 18436
  45.7 33.6 %copy-start = (f32[192,1536]{1,0:T(8,128)}, f32[192,1536]{1,0:T(8,128)S(1)}, u32[]{:S(2)}) copy-start(f32[192,1536]{1,0:T(8,128)S(1)} %bitcast_multiply_fusion) | copy-start | bytes 3538948
  86.1 2.4 copy-start.3
  89.6 2.4 copy-start.7
  91.7 1.2 copy-start.5
  92.9 2.4 copy-start.6
  95.6 1.7 copy-start.1
  95.7 1.0 copy-start.8
  102.6 1.3 copy-start.2
  113.8 167.0 %all-to-all-start.1 = ((bf16[64,3,2560]{2,1,0:T(4,128)(2,1)}), bf16[64,3,2560]{2,1,0:T(4,128)(2,1)S(1)}, u32[]{:S(2)}, u32[]{:S(2)}) async-start(bf16[64,3,2560]{2,1,0:T(4,128)(2,1)} %maximum_bitcast_fusion), calls=%async_computation.1 | async-start | bytes 2621440 | tf_op jit(solution)/shard_map/all_to_all | solution.py:105
  120.8 162.3 %reduce-scatter.7.cloned.1.call-start = ((), (), s32[]{:S(2)}) async-start(), calls=%async_computation.6 | async-start | bytes 884736
Sparse Core Ops, SparseCore 0:
  10.5 63.0 all-gather.1
  102.5 102.4 reduce-scatter.4
  207.5 37.9 reduce-scatter.6

commit v2 on v1

--- a/solution.py
+++ b/solution.py
@@ -83,19 +83,25 @@
         ],
         axis=1,
     )
-    product = lax.dot_general(
-        scaled, qkv_grad, (((0,), (0,)), ((), ())), preferred_element_type=jnp.float32
+    frame_count = lax.axis_size("frame")
+    col_block = 3 * inner // joint_count
+    product = jnp.einsum(
+        "tk,tjc->jkc",
+        scaled,
+        qkv_grad.reshape(count, joint_count, col_block),
+        preferred_element_type=jnp.float32,
     )
-    frame_sum = lax.psum_scatter(
-        (product * grad_scale).astype(jnp.bfloat16), "frame", scatter_dimension=0, tiled=True
-    )
-    joint_part = lax.psum_scatter(frame_sum, "joint", scatter_dimension=1, tiled=True)
-    weight_grad = lax.all_gather(joint_part, "joint", axis=1, tiled=True).astype(jnp.float32)
+    product = (product * grad_scale).astype(jnp.bfloat16)
+    product = product.reshape(joint_count * frame_count, width // frame_count, col_block)
+    block = lax.psum_scatter(product, ("joint", "frame"), scatter_dimension=0, tiled=True)
+    weight_grad = lax.all_gather(block, "joint", axis=0, tiled=True)
+    weight_grad = weight_grad.transpose(1, 0, 2).reshape(width // frame_count, 3 * inner)
+    weight_grad = weight_grad.astype(jnp.float32)
     normed_grad = lax.dot_general(
         qkv_grad, whole, (((1,), (1,)), ((), ())), preferred_element_type=jnp.float32
     )
     gain_part = jnp.sum(normed_grad * normed, axis=0) * grad_scale
-    gain_grad = lax.psum(gain_part, ("joint", "frame"))
+    gain_grad = lax.psum(lax.psum(gain_part, "frame"), "joint")
     upper = normed_grad * norm_gain
     token_grad = rinv * (upper - normed * jnp.mean(upper * normed, axis=1, keepdims=True))
     token_grad = token_grad.astype(jnp.bfloat16).reshape(local_frames, joints, width)

time: 319 us -> 552 us (1.73)
  waiting for transfers between devices: 113 us -> 331 us
  local copies, waits for them, and re-layouts: 14.4 us -> 24.7 us
  blocking collectives: 134 us -> 140 us
    reduce_scatter x1, waiting for transfers between devices: 84.1 us -> 304 us  [per_device(): lax.psum_scatter(product, ('joint', 'frame'), scatter_dimension=0, tiled=...]
    convert_element_type x0 -> x2, local copies, waits for them, and re-layouts: none -> 13.5 us  [the longest x1 12.7 us: per_device(): product = (product * grad_scale).astype(jnp.bfloat16)]
    psum x1 -> x2, blocking collectives: 73.7 us -> 79.1 us  [per_device(): gain_grad = lax.psum(lax.psum(gain_part, 'frame'), 'joint')]
  transfers between devices with their start and end apart: 4 -> 3, of which waited for: 2 -> 2; matrix products, arithmetic and copies ran while one was open for 5% -> 3% of each run, Pallas kernels for 0% -> 0%
where the time goes in v2:
time: 552 us
  waiting for transfers between devices  331 us (60%)
  blocking collectives  140 us (25%)
  matrix products  28.2 us (5%)
  local copies, waits for them, and re-layouts  24.7 us (4%)
  between operations  14.3 us (3%)
  starting transfers between devices  7.08 us (1%)
  other arithmetic  6.08 us (1%)
    reduce_scatter x1, waiting for transfers between devices, per_device(): lax.psum_scatter(product, ('joint', 'frame'), scatter_dimension=0, tiled=...  304 us
    psum x2, blocking collectives, per_device(): gain_grad = lax.psum(lax.psum(gain_part, 'frame'), 'joint')  79.1 us
    all_to_all x1, blocking collectives, per_device(): packed = lax.all_to_all(packed, 'joint', 1, 0, tiled=True)  35.6 us
    all_gather x1, waiting for transfers between devices, per_device(): whole = lax.all_gather(qkv_weight, 'frame', axis=0, tiled=True)  26.6 us
    all_gather x1, blocking collectives, per_device(): weight_grad = lax.all_gather(block, 'joint', axis=0, tiled=True)  25 us
    convert_element_type x1, local copies, waits for them, and re-layouts, per_device(): product = (product * grad_scale).astype(jnp.bfloat16)  12.7 us
  transfers between devices with their start and end apart: 3, of which 2 were waited for; matrix products, arithmetic and copies ran while one was open for 3% of the time, Pallas kernels for 0%

profile of v2, /device:TPU:2, one launch (start us, length us, event | category | flops | bytes accessed | tf_op | source)
XLA Modules:
  0.0 551.6 jit_solution(3843800422957755215)
XLA Ops:
  7.2 0.0 copy-start.3
  7.2 0.0 all-gather.2.cloned.1.call-start
  7.2 0.7 all-gather.2.cloned.1.call-update
  7.9 0.0 reduce-scatter.2.cloned.1.call-start
  8.0 1.2 copy.85
  9.2 0.0 copy-done.3
  9.2 0.2 copy.84
  9.4 0.1 pad_maximum_fusion
  9.4 35.6 %all_to_all.36 = bf16[8,24,2560]{2,0,1:T(8,128)(2,1)S(1)} all-to-all(bf16[8,24,2560]{2,0,1:T(8,128)(2,1)S(1)} %pad_maximum_fusion), channel_id=1, replica_groups=mesh['joint'=8,'frame'=32] {'joint'}, dimensions={1} | all-to-all | bytes 1966080 | tf_op jit(solution)/shard_map/all_to_all | solution.py:62
  45.0 0.1 copy.166
  45.1 0.2 multiply_reduce_fusion.2
  45.3 0.1 rsqrt.13
  45.4 0.3 copy-done.9
  45.7 1.0 multiply_convert_fusion.1
  46.7 0.1 slice_convert_fusion
  46.9 0.1 bitcast_multiply_fusion
  47.0 0.0 copy-start
  47.0 26.6 %all-gather.2.cloned.1.call-done = bf16[1536,3072]{1,0:T(8,128)(2,1)} async-done(((bf16[48,3072]{1,0:T(8,128)(2,1)}), bf16[1536,3072]{1,0:T(8,128)(2,1)}) %all-gather.2.cloned.1.call-update) | async-done | bytes 9437200 | tf_op jit(solution)/shard_map/all_gather | solution.py:59
  73.6 5.7 %fusion.4 = bf16[24,8,24,128]{3,1,2,0:T(8,128)(2,1)S(1)} fusion(bf16[1536,3072]{1,0:T(8,128)(2,1)} %all-gather.2.cloned.1.call-done, f32[192,1536]{1,0:T(8,128)S(1)} %bitcast_multiply_fusion, f32[1536]{0:T(1024)S(1)} %copy-done.9), kind=kOutput, calls=%fused_computation.8 | convolution fusion | flops 1813118976 | bytes 11802624 | tf_op jit(solution)/shard_map/dot_general | solution.py:70
  79.3 0.2 copy.122
  79.6 1.1 fusion.31
  80.7 0.3 fusion.16
  81.0 2.4 fusion.32
  83.4 2.7 fusion.11
  86.1 2.4 fusion.9
  88.5 0.1 fusion.30
  88.6 0.9 copy.99
  89.6 2.1 convert_reduce_fusion
  91.7 0.0 copy-start.5
  91.7 0.3 copy.101
  92.0 0.9 copy.95
  92.9 2.1 convert_reduce_fusion.1
  95.0 0.3 copy.98
  95.3 0.0 copy-done.6
  95.3 0.3 copy.94
  95.6 0.0 copy-start.4
  95.6 0.1 bitcast_dynamic-update-slice_fusion.2
  95.6 0.1 bitcast_dynamic-update-slice_fusion.1
  95.7 0.1 bitcast_dynamic-update-slice_fusion
  95.8 1.1 copy-done.8
  96.8 0.0 copy-done.4
  96.8 5.2 fusion.2
  102.0 12.7 %copy.107 = bf16[8,1536,384]{2,1,0:T(8,128)(2,1)} copy(bf16[8,1536,384]{1,2,0:T(8,128)(2,1)} %fusion.2) | data formatting | bytes 18874368 | tf_op jit(solution)/shard_map/convert_element_type | solution.py:94
  114.7 0.0 reduce-scatter.2.cloned.1.call-update
  114.7 0.3 fusion.10
  115.0 0.0 copy-start.1
  115.0 0.3 copy.113
  115.3 0.1 reshape.96
  115.4 0.9 copy-done.1
  116.3 7.4 %multiply_reduce_fusion = (f32[1536]{0:T(1024)S(1)}, f32[192]{0:T(256)S(1)}, f32[192,1536]{1,0:T(8,128)S(1)}) fusion(f32[192,1536]{1,0:T(8,128)S(1)} %copy-done.1, f32[1536]{0:T(1024)S(1)} %copy-done.9, bf16[192,3072]{1,0:T(8,128)(2,1)} %copy-done.8, bf16[1536,3072]{1,0:T(8,128)(2,1)} %all-gather.2.cloned.1.call-done), kind=kOutput, calls=%fused_computation.23 | convolution fusion | flops 1813412096 | bytes 12989184 | tf_op jit(solution)/shard_map/dot_general | solution.py:100
  123.7 0.3 multiply_convert_fusion.2
  124.0 0.5 copy.103
  124.5 1.7 maximum_bitcast_fusion
  126.2 7.0 %all-to-all-start.1 = ((bf16[64,3,2560]{2,1,0:T(4,128)(2,1)}), bf16[64,3,2560]{2,1,0:T(4,128)(2,1)S(1)}, u32[]{:S(2)}, u32[]{:S(2)}) async-start(bf16[64,3,2560]{2,1,0:T(4,128)(2,1)} %maximum_bitcast_fusion), calls=%async_computation.1 | async-start | bytes 2621440 | tf_op jit(solution)/shard_map/all_to_all | solution.py:111
  133.2 61.7 %psum.14 = f32[1536]{0:T(1024)S(1)} all-reduce(f32[1536]{0:T(1024)S(1)} %broadcast_multiply_fusion), channel_id=1, replica_groups=mesh['joint'=8,'frame'=32] {'frame'}, use_global_device_ids=true, to_apply=%region_9.0 | all-reduce | flops 1536 | bytes 12288 | tf_op jit(solution)/shard_map/psum | solution.py:104
  194.9 17.3 %psum.15 = f32[1536]{0:T(1024)} all-reduce(f32[1536]{0:T(1024)S(1)} %psum.14), channel_id=1, replica_groups=mesh['joint'=8,'frame'=32] {'joint'}, use_global_device_ids=true, to_apply=%region_10.0 | all-reduce | flops 1536 | bytes 12288 | tf_op jit(solution)/shard_map/psum | solution.py:104
  212.3 0.0 all-to-all-done.1
  212.3 0.2 copy.165
  212.5 0.1 copy.105
  212.7 1.0 copy.110
  213.7 1.0 copy.109
  214.6 304.2 %reduce-scatter.2.cloned.1.call-done = bf16[1,48,384]{2,1,0:T(8,128)(2,1)} async-done(((bf16[256,48,384]{2,1,0:T(8,128)(2,1)}), bf16[1,48,384]{2,1,0:T(8,128)(2,1)}) %reduce-scatter.2.cloned.1.call-update) | async-done | bytes 36880 | tf_op jit(solution)/shard_map/reduce_scatter | solution.py:96
  518.8 25.0 %all_gather.7 = bf16[8,48,384]{2,1,0:T(8,128)(2,1)S(1)} all-gather(bf16[1,48,384]{2,1,0:T(8,128)(2,1)} %reduce-scatter.2.cloned.1.call-done), channel_id=1, replica_groups=mesh['joint'=8,'frame'=32] {'joint'}, dimensions={0}, use_global_device_ids=true | all-gather | bytes 331776 | tf_op jit(solution)/shard_map/all_gather | solution.py:97
  543.9 0.9 copy.121
  (15 shorter events, 0.2 us)
Async XLA Ops:
  7.2 2.0 copy-start.3
  7.2 66.5 %all-gather.2.cloned.1.call-start = ((), (), s32[]{:S(2)}) async-start(), calls=%async_computation.3 | async-start | bytes 9732096 | tf_op jit(solution)/shard_map/all_gather | solution.py:59
  7.9 510.9 %reduce-scatter.2.cloned.1.call-start = ((), (), s32[]{:S(2)}) async-start(), calls=%async_computation.4 | async-start | bytes 9474048 | tf_op jit(solution)/shard_map/reduce_scatter | solution.py:96
  45.0 0.7 copy-start.9
  47.0 32.3 %copy-start = (f32[192,1536]{1,0:T(8,128)}, f32[192,1536]{1,0:T(8,128)S(1)}, u32[]{:S(2)}) copy-start(f32[192,1536]{1,0:T(8,128)S(1)} %bitcast_multiply_fusion) | copy-start | bytes 3538948
  86.1 2.4 copy-start.2
  89.6 2.4 copy-start.7
  91.7 1.2 copy-start.5
  92.9 2.4 copy-start.6
  95.6 1.3 copy-start.4
  95.7 1.1 copy-start.8
  115.0 1.3 copy-start.1
  126.2 86.1 %all-to-all-start.1 = ((bf16[64,3,2560]{2,1,0:T(4,128)(2,1)}), bf16[64,3,2560]{2,1,0:T(4,128)(2,1)S(1)}, u32[]{:S(2)}, u32[]{:S(2)}) async-start(bf16[64,3,2560]{2,1,0:T(4,128)(2,1)} %maximum_bitcast_fusion), calls=%async_computation.1 | async-start | bytes 2621440 | tf_op jit(solution)/shard_map/all_to_all | solution.py:111
Sparse Core Ops, SparseCore 0:
  10.5 63.0 all-gather.1
  114.8 403.9 reduce-scatter.1

commit v3 on v1

--- a/solution.py
+++ b/solution.py
@@ -49,24 +49,40 @@
     joint_rows, frame_rows, width = tokens.shape
     inner = out_grad.shape[2]
     joint_count = lax.axis_size("joint")
-    total_tokens = joint_rows * frame_rows * joint_count * lax.axis_size("frame")
+    chips = lax.axis_size("chip")
+    cores = lax.axis_size("core")
+    total_tokens = joint_rows * frame_rows * joint_count * chips * cores
     grad_scale = 1.0 / math.sqrt(total_tokens)
     inv_root = 1.0 / math.sqrt(HDIM)
     joints = joint_rows * joint_count
     local_frames = frame_rows // joint_count
     count = joints * local_frames
 
-    whole = lax.all_gather(qkv_weight, "frame", axis=0, tiled=True)
+    whole = lax.all_gather(qkv_weight, "chip", axis=0, tiled=True)
+    whole = lax.all_gather(whole, "core", axis=0, tiled=True)
+    rows = width // (chips * cores)
+
+    def to_fine(x):
+        lead = x.shape[:-1]
+        x = x.reshape(lead + (chips, cores, rows))
+        return jnp.swapaxes(x, -3, -2).reshape(lead + (width,))
+
+    def from_fine(x):
+        lead = x.shape[:-1]
+        x = x.reshape(lead + (cores, chips, rows))
+        return jnp.swapaxes(x, -3, -2).reshape(lead + (width,))
+
+    gain_fine = to_fine(norm_gain)
 
     packed = jnp.concatenate([tokens, out_grad], axis=2)
     packed = lax.all_to_all(packed, "joint", 1, 0, tiled=True)
     packed = packed.transpose(1, 0, 2)
-    flat = packed[:, :, :width].reshape(count, width).astype(jnp.float32)
+    flat = to_fine(packed[:, :, :width].reshape(count, width)).astype(jnp.float32)
     upstream = packed[:, :, width:].reshape(local_frames, joints, HEADS, HDIM)
 
     rinv = lax.rsqrt(jnp.mean(flat * flat, axis=1, keepdims=True) + EPSILON)
     normed = flat * rinv
-    scaled = (normed * norm_gain).astype(jnp.bfloat16)
+    scaled = (normed * gain_fine).astype(jnp.bfloat16)
     projected = jnp.dot(scaled, whole, preferred_element_type=jnp.float32).astype(jnp.bfloat16)
     projected = projected.reshape(local_frames, joints, 3, HEADS, HDIM)
     queries = projected[:, :, 0]
@@ -86,19 +102,19 @@
     product = lax.dot_general(
         scaled, qkv_grad, (((0,), (0,)), ((), ())), preferred_element_type=jnp.float32
     )
-    frame_sum = lax.psum_scatter(
-        (product * grad_scale).astype(jnp.bfloat16), "frame", scatter_dimension=0, tiled=True
-    )
+    part = (product * grad_scale).astype(jnp.bfloat16)
+    part = lax.psum_scatter(part, "core", scatter_dimension=0, tiled=True)
+    frame_sum = lax.psum_scatter(part, "chip", scatter_dimension=0, tiled=True)
     joint_part = lax.psum_scatter(frame_sum, "joint", scatter_dimension=1, tiled=True)
     weight_grad = lax.all_gather(joint_part, "joint", axis=1, tiled=True).astype(jnp.float32)
     normed_grad = lax.dot_general(
         qkv_grad, whole, (((1,), (1,)), ((), ())), preferred_element_type=jnp.float32
     )
     gain_part = jnp.sum(normed_grad * normed, axis=0) * grad_scale
-    gain_grad = lax.psum(gain_part, ("joint", "frame"))
-    upper = normed_grad * norm_gain
+    gain_grad = from_fine(lax.psum(gain_part, ("joint", "chip", "core")))
+    upper = normed_grad * gain_fine
     token_grad = rinv * (upper - normed * jnp.mean(upper * normed, axis=1, keepdims=True))
-    token_grad = token_grad.astype(jnp.bfloat16).reshape(local_frames, joints, width)
+    token_grad = from_fine(token_grad.astype(jnp.bfloat16)).reshape(local_frames, joints, width)
     back = jnp.concatenate(
         [attended.reshape(local_frames, joints, inner), token_grad], axis=2
     ).transpose(1, 0, 2)
@@ -109,11 +125,16 @@
 
 
 def solution(mesh):
-    placed = (P("joint", "frame", None), P(), P("frame", None), P("joint", "frame", None))
+    joint_count, frame_count = mesh.devices.shape
+    fine = jax.sharding.Mesh(
+        mesh.devices.reshape(joint_count, frame_count // 2, 2), ("joint", "chip", "core")
+    )
+    frame = ("chip", "core")
+    placed = (P("joint", frame, None), P(), P(frame, None), P("joint", frame, None))
     return jax.shard_map(
         per_device,
-        mesh=mesh,
+        mesh=fine,
         in_specs=placed,
-        out_specs=(P("joint", "frame", None), P("joint", "frame", None), P("frame", None), P()),
+        out_specs=(P("joint", frame, None), P("joint", frame, None), P(frame, None), P()),
         check_vma=False,
     )

time: 319 us -> 373 us (1.17)
  waiting for transfers between devices: 113 us -> 175 us
  blocking collectives: 134 us -> 98.9 us
  local copies, waits for them, and re-layouts: 14.4 us -> 34.4 us
  starting transfers between devices: 7.13 us -> 14.5 us
    all_gather x1 -> x2, waiting for transfers between devices: 27.9 us -> 64.3 us  [the longest x1 64.2 us: per_device(): whole = lax.all_gather(qkv_weight, 'chip', axis=0, tiled=True)]
    all_to_all x1 -> x0, blocking collectives: 35.6 us -> none  [per_device(): packed = lax.all_to_all(packed, 'joint', 1, 0, tiled=True)]
    all_to_all x0 -> x1, waiting for transfers between devices: none -> 26.9 us  [per_device(): packed = lax.all_to_all(packed, 'joint', 1, 0, tiled=True)]
    convert_element_type x0 -> x4, local copies, waits for them, and re-layouts: none -> 12.5 us  [the longest x3 12.3 us: per_device(): to_fine(packed[:, :, :width].reshape(count, width)).astype(jnp.float32)]
    all_to_all x0 -> x1, starting transfers between devices: none -> 7.14 us  [per_device(): packed = lax.all_to_all(packed, 'joint', 1, 0, tiled=True)]
    transpose x0 -> x4, local copies, waits for them, and re-layouts: none -> 3.95 us  [the longest x2 2.04 us: from_fine(): return jnp.swapaxes(x, -3, -2).reshape(lead + (width,))]
    reduce_scatter x1 -> x2, waiting for transfers between devices: 84.1 us -> 82.8 us  [the longest x1 65.7 us: per_device(): frame_sum = lax.psum_scatter(part, 'chip', scatter_dimension=0, tiled=True)]
    unnamed x29 -> x31, local copies, waits for them, and re-layouts: 9.18 us -> 10.3 us
  transfers between devices with their start and end apart: 4 -> 7, of which waited for: 2 -> 4; matrix products, arithmetic and copies ran while one was open for 5% -> 9% of each run, Pallas kernels for 0% -> 0%
where the time goes in v3:
time: 373 us; the launch traced here: 371 us
  waiting for transfers between devices  175 us (47%)
  blocking collectives  98.9 us (27%)
  local copies, waits for them, and re-layouts  34.4 us (9%)
  matrix products  28 us (8%)
  starting transfers between devices  14.5 us (4%)
  between operations  14.1 us (4%)
  other arithmetic  6.12 us (2%)
    psum x1, blocking collectives, per_device(): gain_grad = from_fine(lax.psum(gain_part, ('joint', 'chip', 'core')))  73.8 us
    reduce_scatter x1, waiting for transfers between devices, per_device(): frame_sum = lax.psum_scatter(part, 'chip', scatter_dimension=0, tiled=True)  65.7 us
    all_gather x1, waiting for transfers between devices, per_device(): whole = lax.all_gather(qkv_weight, 'chip', axis=0, tiled=True)  64.2 us
    all_to_all x1, waiting for transfers between devices, per_device(): packed = lax.all_to_all(packed, 'joint', 1, 0, tiled=True)  26.9 us
    all_gather x1, blocking collectives, per_device(): lax.all_gather(joint_part, 'joint', axis=1, tiled=True).astype(jnp.float32)  25.1 us
    reduce_scatter x1, waiting for transfers between devices, per_device(): part = lax.psum_scatter(part, 'core', scatter_dimension=0, tiled=True)  17.2 us
    convert_element_type x3, local copies, waits for them, and re-layouts, per_device(): to_fine(packed[:, :, :width].reshape(count, width)).astype(jnp.float32)  12.3 us
    unnamed x31, local copies, waits for them, and re-layouts  10.3 us
  transfers between devices with their start and end apart: 7, of which 4 were waited for; matrix products, arithmetic and copies ran while one was open for 9% of the time, Pallas kernels for 0%

profile of v3, /device:TPU:2, one launch (start us, length us, event | category | flops | bytes accessed | tf_op | source)
XLA Modules:
  0.0 370.8 jit_solution(7533253656647642720)
XLA Ops:
  7.2 0.7 all-gather.3.cloned.1.call-update
  7.9 64.2 %all-gather.3.cloned.1.call-done = bf16[768,3072]{1,0:T(8,128)(2,1)} async-done(((bf16[48,3072]{1,0:T(8,128)(2,1)}), bf16[768,3072]{1,0:T(8,128)(2,1)}) %all-gather.3.cloned.1.call-update) | async-done | bytes 4718608 | tf_op jit(solution)/shard_map/all_gather | solution.py:61
  72.2 1.0 copy-done.5
  73.2 0.2 copy.95
  73.4 0.8 copy-done.3
  74.3 0.2 copy.94
  74.4 1.0 pad_maximum_fusion
  75.5 7.1 %all-to-all-start = ((bf16[8,24,2560]{2,0,1:T(8,128)(2,1)}), bf16[8,24,2560]{2,0,1:T(8,128)(2,1)S(1)}, u32[]{:S(2)}, u32[]{:S(2)}) async-start(bf16[8,24,2560]{2,0,1:T(8,128)(2,1)} %pad_maximum_fusion), calls=%async_computation | async-start | bytes 1966080 | tf_op jit(solution)/shard_map/all_to_all | solution.py:78
  82.7 0.1 reshape.68
  82.8 0.1 mul.77
  82.8 26.9 %all-to-all-done = bf16[8,24,2560]{2,0,1:T(8,128)(2,1)S(1)} async-done(((bf16[8,24,2560]{2,0,1:T(8,128)(2,1)}), bf16[8,24,2560]{2,0,1:T(8,128)(2,1)S(1)}, u32[]{:S(2)}, u32[]{:S(2)}) %all-to-all-start) | async-done | bytes 983072 | tf_op jit(solution)/shard_map/all_to_all | solution.py:78
  109.8 0.1 copy.175
  109.9 0.2 multiply_reduce_fusion.2
  110.1 0.1 reshape.85
  110.2 0.7 copy-done
  110.8 1.2 slice_convert_fusion
  112.0 6.0 %reshape.86 = f32[192,16,2,48]{3,2,1,0:T(2,128)S(1)} reshape(f32[3,64,1536]{2,1,0:T(8,128)} %slice_convert_fusion) | data formatting | bytes 2359296 | tf_op jit(solution)/shard_map/convert_element_type | solution.py:80
  118.0 4.4 %copy.97 = f32[192,2,16,48]{0,3,2,1:T(8,128)} copy(f32[192,2,16,48]{3,1,2,0:T(2,128)S(1)} %bitcast.99) | data formatting | bytes 2359296 | tf_op jit(solution)/shard_map/convert_element_type | solution.py:80
  122.4 1.9 copy.98
  124.3 5.8 %fusion.3 = bf16[24,8,24,128]{3,1,2,0:T(8,128)(2,1)S(1)} fusion(bf16[1536,3072]{1,0:T(8,128)(2,1)} %all-gather.5.cloned.1.call-done, f32[192,1536]{1,0:T(8,128)S(1)} %copy.98, f32[1536]{0:T(1024)S(1)} %mul.77, f32[192]{0:T(256)S(1)} %reshape.85), kind=kOutput, calls=%fused_computation.7 | convolution fusion | flops 1813413888 | bytes 11803392 | tf_op jit(solution)/shard_map/dot_general | solution.py:86
  130.1 0.2 copy.134
  130.3 1.1 fusion.27
  131.4 0.2 copy-done.1
  131.6 0.3 fusion.12
  131.9 2.4 fusion.28
  134.3 2.7 fusion.10
  137.0 2.4 fusion.8
  139.4 0.1 fusion.26
  139.5 0.9 copy.112
  140.5 2.1 convert_reduce_fusion
  142.6 0.3 copy.115
  142.9 0.9 copy.108
  143.8 2.1 convert_reduce_fusion.1
  145.9 0.3 copy.111
  146.2 0.3 copy.107
  146.5 0.1 bitcast_dynamic-update-slice_fusion.2
  146.5 0.1 bitcast_dynamic-update-slice_fusion.1
  146.6 1.0 copy-done.8
  147.6 5.2 %multiply_convert_fusion = bf16[1536,3072]{1,0:T(8,128)(2,1)} fusion(bf16[192,3072]{1,0:T(8,128)(2,1)S(1)} %bitcast_dynamic-update-slice_fusion, f32[192,1536]{1,0:T(8,128)S(1)} %copy.98, f32[1536]{0:T(1024)S(1)} %mul.77, f32[192]{0:T(256)S(1)} %reshape.85), kind=kOutput, calls=%fused_computation.2 | convolution fusion | flops 1822261248 | bytes 11803392 | tf_op jit(solution)/shard_map/dot_general | solution.py:102
  152.8 0.2 reduce-scatter.8.cloned.1.call-start
  153.1 17.2 %reduce-scatter.6.cloned.1.call-done = bf16[768,3072]{1,0:T(8,128)(2,1)} async-done(((bf16[1536,3072]{1,0:T(8,128)(2,1)}), bf16[768,3072]{1,0:T(8,128)(2,1)}) %reduce-scatter.6.cloned.1.call-update) | async-done | bytes 4718608 | tf_op jit(solution)/shard_map/reduce_scatter | solution.py:106
  170.2 0.3 fusion.9
  170.6 0.1 copy.176
  170.7 0.8 copy-done.9
  171.5 7.1 %multiply_reduce_fusion = (f32[1536]{0:T(1024)S(1)}, f32[192]{0:T(256)S(1)}, f32[192,1536]{1,0:T(8,128)S(1)}) fusion(f32[192,1536]{1,0:T(8,128)S(1)} %copy.98, f32[192]{0:T(256)S(1)} %reshape.85, f32[1536]{0:T(1024)S(1)} %mul.77, bf16[192,3072]{1,0:T(8,128)(2,1)S(1)} %copy-done.9, bf16[1536,3072]{1,0:T(8,128)(2,1)} %all-gather.5.cloned.1.call-done), kind=kOutput, calls=%fused_computation.18 | convolution fusion | flops 1813707008 | bytes 12989952 | tf_op jit(solution)/shard_map/dot_general | solution.py:110
  178.6 0.3 multiply_convert_fusion.1
  178.9 0.3 copy.116
  179.2 2.0 copy.117
  181.2 2.8 reshape_reshape.8
  184.1 0.1 maximum_bitcast_fusion
  184.1 1.9 copy.118
  186.0 7.0 %all-to-all-start.1 = ((bf16[64,3,2560]{2,1,0:T(4,128)(2,1)}), bf16[64,3,2560]{2,1,0:T(4,128)(2,1)S(1)}, u32[]{:S(2)}, u32[]{:S(2)}) async-start(bf16[64,3,2560]{2,1,0:T(4,128)(2,1)} %copy.118), calls=%async_computation.1 | async-start | bytes 2621440 | tf_op jit(solution)/shard_map/all_to_all | solution.py:121
  193.1 65.7 %reduce-scatter.8.cloned.1.call-done = bf16[48,3072]{1,0:T(8,128)(2,1)} async-done(((bf16[768,3072]{1,0:T(8,128)(2,1)}), bf16[48,3072]{1,0:T(8,128)(2,1)}) %reduce-scatter.8.cloned.1.call-update) | async-done | bytes 294928 | tf_op jit(solution)/shard_map/reduce_scatter | solution.py:107
  258.8 2.2 copy.126
  261.0 0.1 reshape.78
  261.1 0.1 reshape.79
  261.2 73.8 %psum.7 = f32[1536]{0:T(1024)} all-reduce(f32[1536]{0:T(1024)S(1)} %reshape.79), channel_id=1, replica_groups=mesh['joint'=8,'chip'=16,'core'=2] {'joint','chip','core'}, use_global_device_ids=true, to_apply=%region_11.0 | all-reduce | flops 1536 | bytes 12288 | tf_op jit(solution)/shard_map/psum | solution.py:114
  335.0 0.2 copy.174
  335.2 0.1 copy.120
  335.4 1.0 copy.123
  336.4 1.0 copy.122
  337.3 1.0 copy.127
  338.3 25.1 %all_gather.11 = bf16[48,3072]{1,0:T(8,128)(2,1)S(1)} all-gather(bf16[48,384]{1,0:T(8,128)(2,1)S(1)} %copy.127), channel_id=1, replica_groups=mesh['joint'=8,'chip'=16,'core'=2] {'joint'}, dimensions={1}, use_global_device_ids=true | all-gather | bytes 331776 | tf_op jit(solution)/shard_map/all_gather | solution.py:109
  363.4 0.9 convert_element_type.79
  (35 shorter events, 0.4 us)
Async XLA Ops:
  7.2 65.0 %all-gather.3.cloned.1.call-start = ((), (), s32[]{:S(2)}) async-start(), calls=%async_computation.5 | async-start | bytes 5013504 | tf_op jit(solution)/shard_map/all_gather | solution.py:61
  7.9 116.4 %all-gather.5.cloned.1.call-start = ((), (), s32[]{:S(2)}) async-start(), calls=%async_computation.6 | async-start | bytes 14155776 | tf_op jit(solution)/shard_map/all_gather | solution.py:62
  72.2 1.0 copy-start.5
  73.2 1.1 copy-start.3
  75.5 7.2 %copy-start.10 = (f32[1536]{0:T(1024)S(1)}, f32[1536]{0:T(1024)}, u32[]{:S(2)}) copy-start(f32[1536]{0:T(1024)} %param.5) | copy-start | bytes 18436
  75.5 34.3 %all-to-all-start = ((bf16[8,24,2560]{2,0,1:T(8,128)(2,1)}), bf16[8,24,2560]{2,0,1:T(8,128)(2,1)S(1)}, u32[]{:S(2)}, u32[]{:S(2)}) async-start(bf16[8,24,2560]{2,0,1:T(8,128)(2,1)} %pad_maximum_fusion), calls=%async_computation | async-start | bytes 1966080 | tf_op jit(solution)/shard_map/all_to_all | solution.py:78
  82.6 87.6 %reduce-scatter.6.cloned.1.call-start = ((), (), s32[]{:S(2)}) async-start(), calls=%async_computation.7 | async-start | bytes 14155776 | tf_op jit(solution)/shard_map/reduce_scatter | solution.py:106
  109.8 1.0 copy-start
  130.3 1.3 copy-start.1
  137.0 2.4 copy-start.2
  140.5 2.4 copy-start.7
  142.6 1.2 copy-start.4
  143.8 2.4 copy-start.6
  146.6 1.0 copy-start.8
  152.8 106.0 %reduce-scatter.8.cloned.1.call-start = ((), (), s32[]{:S(2)}) async-start(), calls=%async_computation.8 | async-start | bytes 5013504 | tf_op jit(solution)/shard_map/reduce_scatter | solution.py:107
  170.2 1.3 copy-start.9
  186.0 149.0 %all-to-all-start.1 = ((bf16[64,3,2560]{2,1,0:T(4,128)(2,1)}), bf16[64,3,2560]{2,1,0:T(4,128)(2,1)S(1)}, u32[]{:S(2)}, u32[]{:S(2)}) async-start(bf16[64,3,2560]{2,1,0:T(4,128)(2,1)} %copy.118), calls=%async_computation.1 | async-start | bytes 2621440 | tf_op jit(solution)/shard_map/all_to_all | solution.py:121
  193.1 144.3 %reduce-scatter.10.cloned.1.call-start = ((), (), s32[]{:S(2)}) async-start(), calls=%async_computation.9 | async-start | bytes 884736
Sparse Core Ops, SparseCore 0:
  10.4 61.7 all-gather.2
  74.0 26.6 all-gather.4
  153.0 17.2 reduce-scatter.5
  173.7 85.0 reduce-scatter.7
  261.2 38.1 reduce-scatter.9

commit v4 on v1

--- a/solution.py
+++ b/solution.py
@@ -5,11 +5,13 @@
 from jax import lax
 from jax.sharding import PartitionSpec as P
 
+
 HEADS = 8
 HDIM = 128
 
 
 EPSILON = 1e-05
+SIDE_COLS = 768
 
 
 def attention_local(queries, keys_all, values_all, upstream, inv_root, groups):
@@ -45,7 +47,7 @@
     return attended, query_grad, key_grad, value_grad
 
 
-def per_device(tokens, norm_gain, qkv_weight, out_grad):
+def per_device_body(tokens, norm_gain, qkv_weight, out_grad):
     joint_rows, frame_rows, width = tokens.shape
     inner = out_grad.shape[2]
     joint_count = lax.axis_size("joint")
@@ -86,16 +88,41 @@
     product = lax.dot_general(
         scaled, qkv_grad, (((0,), (0,)), ((), ())), preferred_element_type=jnp.float32
     )
-    frame_sum = lax.psum_scatter(
-        (product * grad_scale).astype(jnp.bfloat16), "frame", scatter_dimension=0, tiled=True
-    )
-    joint_part = lax.psum_scatter(frame_sum, "joint", scatter_dimension=1, tiled=True)
-    weight_grad = lax.all_gather(joint_part, "joint", axis=1, tiled=True).astype(jnp.float32)
+    frame_count = lax.axis_size("frame")
+    row_count = width // frame_count
+    col_block = 3 * inner // joint_count
+    ring_cols = 3 * inner - SIDE_COLS
+    part = (product * grad_scale).astype(jnp.bfloat16)
+    ring_sum = lax.psum_scatter(part[:, :ring_cols], "frame", scatter_dimension=0, tiled=True)
     normed_grad = lax.dot_general(
         qkv_grad, whole, (((1,), (1,)), ((), ())), preferred_element_type=jnp.float32
     )
-    gain_part = jnp.sum(normed_grad * normed, axis=0) * grad_scale
-    gain_grad = lax.psum(gain_part, ("joint", "frame"))
+    gain_part = (jnp.sum(normed_grad * normed, axis=0) * grad_scale).reshape(row_count, width // row_count)
+    gain_high = gain_part.astype(jnp.bfloat16)
+    gain_low = (gain_part - gain_high.astype(jnp.float32)).astype(jnp.bfloat16)
+    side = jnp.concatenate(
+        [
+            part[:, ring_cols:].reshape(frame_count, row_count, SIDE_COLS),
+            jnp.broadcast_to(gain_high[None], (frame_count,) + gain_high.shape),
+            jnp.broadcast_to(gain_low[None], (frame_count,) + gain_low.shape),
+        ],
+        axis=2,
+    )
+    side = lax.all_to_all(side, "frame", 0, 0, tiled=True)
+    side = jnp.sum(side.astype(jnp.float32), axis=0)
+    gain_cols = width // row_count
+    side_sum = side[:, :SIDE_COLS]
+    gain_sum = side[:, SIDE_COLS:SIDE_COLS + gain_cols] + side[:, SIDE_COLS + gain_cols:]
+    frame_sum = jnp.concatenate([ring_sum.astype(jnp.float32), side_sum], axis=1)
+    blocks = frame_sum.reshape(row_count, joint_count, col_block).transpose(1, 0, 2)
+    first = (lax.broadcasted_iota(jnp.int32, (joint_count, 1, 1), 0) == 0).astype(jnp.float32)
+    blocks = jnp.concatenate([blocks, first * gain_sum[None]], axis=2)
+    blocks = lax.all_to_all(blocks, "joint", 0, 0, tiled=True)
+    block_sum = jnp.sum(blocks, axis=0)
+    spread = jnp.broadcast_to(block_sum[None], (joint_count,) + block_sum.shape)
+    spread = lax.all_to_all(spread, "joint", 0, 0, tiled=True)
+    weight_grad = spread[:, :, :col_block].transpose(1, 0, 2).reshape(row_count, 3 * inner)
+    gain_grad = spread[0, :, col_block:].reshape(width)
     upper = normed_grad * norm_gain
     token_grad = rinv * (upper - normed * jnp.mean(upper * normed, axis=1, keepdims=True))
     token_grad = token_grad.astype(jnp.bfloat16).reshape(local_frames, joints, width)
@@ -111,7 +138,7 @@
 def solution(mesh):
     placed = (P("joint", "frame", None), P(), P("frame", None), P("joint", "frame", None))
     return jax.shard_map(
-        per_device,
+        per_device_body,
         mesh=mesh,
         in_specs=placed,
         out_specs=(P("joint", "frame", None), P("joint", "frame", None), P("frame", None), P()),

time: 319 us -> 302 us (0.947)
  blocking collectives: 134 us -> 35.6 us
  waiting for transfers between devices: 113 us -> 170 us
  starting transfers between devices: 7.13 us -> 20.1 us
  local copies, waits for them, and re-layouts: 14.4 us -> 22.8 us
  other arithmetic: 5.87 us -> 10.6 us
  matrix products: 28.2 us -> 23.7 us
    all_to_all x1 -> x4, waiting for transfers between devices: 0.01 us -> 102 us  [the longest x1 34.2 us: per_device_body(): side = lax.all_to_all(side, 'frame', 0, 0, tiled=True)]
    psum x1 -> x0, blocking collectives: 73.7 us -> none  [per_device(): gain_grad = lax.psum(gain_part, ('joint', 'frame'))]
    reduce_scatter x1, waiting for transfers between devices: 84.1 us -> 40.8 us  [per_device_body(): lax.psum_scatter(part[:, :ring_cols], 'frame', scatter_dimension=0, tiled...]
    all_gather x1 -> x0, blocking collectives: 25.1 us -> none  [per_device(): lax.all_gather(joint_part, 'joint', axis=1, tiled=True).astype(jnp.float32)]
    all_to_all x1 -> x4, starting transfers between devices: 7.01 us -> 20 us  [the longest x1 7.14 us: per_device_body(): blocks = lax.all_to_all(blocks, 'joint', 0, 0, tiled=True)]
    unnamed x29 -> x40, local copies, waits for them, and re-layouts: 9.18 us -> 12.9 us
    slice x3 -> x8, local copies, waits for them, and re-layouts: 1.19 us -> 4.62 us  [the longest x1 3.54 us: per_device_body(): part[:, :ring_cols]]
  transfers between devices with their start and end apart: 4 -> 6, of which waited for: 2 -> 6; matrix products, arithmetic and copies ran while one was open for 5% -> 7% of each run, Pallas kernels for 0% -> 0%
where the time goes in v4:
time: 302 us; the launch traced here: 297 us
  waiting for transfers between devices  170 us (56%)
  blocking collectives  35.6 us (12%)
  matrix products  23.7 us (8%)
  local copies, waits for them, and re-layouts  22.8 us (8%)
  starting transfers between devices  20.1 us (7%)
  between operations  14.5 us (5%)
  other arithmetic  10.6 us (4%)
    reduce_scatter x1, waiting for transfers between devices, per_device_body(): lax.psum_scatter(part[:, :ring_cols], 'frame', scatter_dimension=0, tiled...  40.8 us
    all_to_all x1, blocking collectives, per_device_body(): packed = lax.all_to_all(packed, 'joint', 1, 0, tiled=True)  35.6 us
    all_to_all x1, waiting for transfers between devices, per_device_body(): side = lax.all_to_all(side, 'frame', 0, 0, tiled=True)  34.2 us
    all_to_all x1, waiting for transfers between devices, per_device_body(): back = lax.all_to_all(back, 'joint', 0, 1, tiled=True)  31.7 us
    all_gather x1, waiting for transfers between devices, per_device_body(): whole = lax.all_gather(qkv_weight, 'frame', axis=0, tiled=True)  26.9 us
    all_to_all x1, waiting for transfers between devices, per_device_body(): spread = lax.all_to_all(spread, 'joint', 0, 0, tiled=True)  19.1 us
    all_to_all x1, waiting for transfers between devices, per_device_body(): blocks = lax.all_to_all(blocks, 'joint', 0, 0, tiled=True)  16.6 us
    unnamed x40, local copies, waits for them, and re-layouts  12.9 us
  transfers between devices with their start and end apart: 6, of which 6 were waited for; matrix products, arithmetic and copies ran while one was open for 7% of the time, Pallas kernels for 0%

profile of v4, /device:TPU:2, one launch (start us, length us, event | category | flops | bytes accessed | tf_op | source)
XLA Modules:
  0.0 297.2 jit_solution(7093252452527347473)
XLA Ops:
  7.2 0.7 all-gather.2.cloned.1.call-update
  8.0 1.2 copy.81
  9.2 0.2 copy.80
  9.4 35.6 %all_to_all.51 = bf16[8,24,2560]{2,0,1:T(8,128)(2,1)S(1)} all-to-all(bf16[8,24,2560]{2,0,1:T(8,128)(2,1)S(1)} %pad_maximum_fusion.1), channel_id=1, replica_groups=mesh['joint'=8,'frame'=32] {'joint'}, dimensions={1} | all-to-all | bytes 1966080 | tf_op jit(solution)/shard_map/all_to_all | solution.py:64
  45.0 0.1 copy.158
  45.1 0.2 multiply_reduce_fusion.2
  45.3 0.1 rsqrt.12
  45.4 0.1 slice_convert_fusion
  45.6 1.0 copy-done
  46.6 0.1 bitcast_multiply_fusion
  46.7 26.9 %all-gather.2.cloned.1.call-done = bf16[1536,3072]{1,0:T(8,128)(2,1)} async-done(((bf16[48,3072]{1,0:T(8,128)(2,1)}), bf16[1536,3072]{1,0:T(8,128)(2,1)}) %all-gather.2.cloned.1.call-update) | async-done | bytes 9437200 | tf_op jit(solution)/shard_map/all_gather | solution.py:61
  73.6 5.7 %fusion.3 = bf16[24,8,24,128]{3,1,2,0:T(8,128)(2,1)S(1)} fusion(bf16[1536,3072]{1,0:T(8,128)(2,1)} %all-gather.2.cloned.1.call-done, f32[192,1536]{1,0:T(8,128)S(1)} %bitcast_multiply_fusion, f32[1536]{0:T(1024)S(1)} %copy-done.14), kind=kOutput, calls=%fused_computation.9 | convolution fusion | flops 1813118976 | bytes 11802624 | tf_op jit(solution)/shard_map/dot_general | solution.py:72
  79.3 0.2 copy.117
  79.6 1.0 fusion.27
  80.5 0.3 fusion.12
  80.9 1.4 fusion.28
  82.3 2.2 fusion.10
  84.5 1.0 fusion.8
  85.4 0.1 fusion.26
  85.5 0.9 copy-done.10
  86.4 0.3 copy.90
  86.7 0.8 bitcast_dynamic-update-slice_fusion.2
  87.5 0.2 copy.91
  87.8 1.0 convert_reduce_fusion.2
  88.8 0.3 copy.94
  89.1 0.2 copy.95
  89.3 1.0 convert_reduce_fusion.1
  90.3 0.3 copy.97
  90.8 1.0 copy-done.12
  91.8 3.1 %multiply_convert_fusion = bf16[1536,3072]{1,0:T(8,128)(2,1)S(1)} fusion(bf16[192,3072]{1,0:T(8,128)(2,1)S(1)} %bitcast_dynamic-update-slice_fusion, f32[192,1536]{1,0:T(8,128)S(1)} %copy-done.4, f32[1536]{0:T(1024)S(1)} %copy-done.14), kind=kOutput, calls=%fused_computation.2 | convolution fusion | flops 1821966336 | bytes 11802624 | tf_op jit(solution)/shard_map/dot_general | solution.py:88
  94.9 3.6 %copy-done.2 = bf16[1536,3072]{1,0:T(8,128)(2,1)} copy-done((bf16[1536,3072]{1,0:T(8,128)(2,1)}, bf16[1536,3072]{1,0:T(8,128)(2,1)S(1)}, u32[]{:S(2)}) %copy-start.2) | copy-done | bytes 9437208
  98.5 3.5 %slice.63 = bf16[1536,2304]{1,0:T(8,128)(2,1)} slice(bf16[1536,3072]{1,0:T(8,128)(2,1)S(1)} %multiply_convert_fusion), slice={[0:1536], [0:2304]} | slice | bytes 14155776 | tf_op jit(solution)/shard_map/slice | solution.py:96
  102.1 1.3 copy-done.5
  103.4 0.4 copy-done.13
  103.7 8.7 %multiply_reduce_fusion = (f32[1536]{0:T(1024)S(1)}, f32[192]{0:T(256)}, f32[192,1536]{1,0:T(8,128)}) fusion(f32[192,1536]{1,0:T(8,128)S(1)} %copy-done.5, f32[1536]{0:T(1024)S(1)} %copy-done.14, bf16[192,3072]{1,0:T(8,128)(2,1)S(1)} %copy-done.13, bf16[1536,3072]{1,0:T(8,128)(2,1)} %all-gather.2.cloned.1.call-done), kind=kOutput, calls=%fused_computation.22 | convolution fusion | flops 1813412096 | bytes 12989184 | tf_op jit(solution)/shard_map/dot_general | solution.py:97
  112.6 1.9 pad_maximum_fusion
  114.5 5.8 %all-to-all-start.2 = ((bf16[32,48,832]{2,1,0:T(8,128)(2,1)}), bf16[32,48,832]{2,1,0:T(8,128)(2,1)S(1)}, u32[]{:S(2)}, u32[]{:S(2)}) async-start(bf16[32,48,832]{2,1,0:T(8,128)(2,1)} %pad_maximum_fusion), calls=%async_computation.3 | async-start | bytes 5505024 | tf_op jit(solution)/shard_map/all_to_all | solution.py:111
  120.3 0.5 compare_convert_fusion
  120.8 0.7 broadcast_multiply_fusion.2
  121.5 34.2 %all-to-all-done.2 = bf16[32,48,832]{2,1,0:T(8,128)(2,1)S(1)} async-done(((bf16[32,48,832]{2,1,0:T(8,128)(2,1)}), bf16[32,48,832]{2,1,0:T(8,128)(2,1)S(1)}, u32[]{:S(2)}, u32[]{:S(2)}) %all-to-all-start.2) | async-done | bytes 2555936 | tf_op jit(solution)/shard_map/all_to_all | solution.py:111
  155.7 0.4 convert_reduce_fusion
  156.2 0.2 copy-done.15
  156.4 0.1 broadcast_multiply_fusion
  156.5 40.8 %reduce-scatter.2.cloned.1.call-done = bf16[48,2304]{1,0:T(8,128)(2,1)} async-done(((bf16[1536,2304]{1,0:T(8,128)(2,1)}), bf16[48,2304]{1,0:T(8,128)(2,1)}) %reduce-scatter.2.cloned.1.call-update) | async-done | bytes 221200 | tf_op jit(solution)/shard_map/reduce_scatter | solution.py:96
  197.2 1.0 convert_element_type.104
  198.3 1.0 pad_maximum_fusion.2
  199.3 7.1 %all-to-all-start.3 = ((f32[8,48,416]{2,1,0:T(8,128)}), f32[8,48,416]{2,1,0:T(8,128)S(1)}, u32[]{:S(2)}, u32[]{:S(2)}) async-start(f32[8,48,416]{2,1,0:T(8,128)} %pad_maximum_fusion.2), calls=%async_computation.4 | async-start | bytes 1572864 | tf_op jit(solution)/shard_map/all_to_all | solution.py:120
  206.5 1.5 multiply_convert_fusion.1
  208.0 0.5 copy.99
  208.5 0.3 fusion.9
  208.9 0.3 copy.108
  209.1 0.1 reshape.110
  209.2 1.7 maximum_bitcast_fusion
  210.9 16.6 %all-to-all-done.3 = f32[8,48,416]{2,1,0:T(8,128)S(1)} async-done(((f32[8,48,416]{2,1,0:T(8,128)}), f32[8,48,416]{2,1,0:T(8,128)S(1)}, u32[]{:S(2)}, u32[]{:S(2)}) %all-to-all-start.3) | async-done | bytes 639008 | tf_op jit(solution)/shard_map/all_to_all | solution.py:120
  227.5 3.6 %all-to-all-start.1 = ((bf16[64,3,2560]{2,1,0:T(4,128)(2,1)}), bf16[64,3,2560]{2,1,0:T(4,128)(2,1)S(1)}, u32[]{:S(2)}, u32[]{:S(2)}) async-start(bf16[64,3,2560]{2,1,0:T(4,128)(2,1)} %maximum_bitcast_fusion), calls=%async_computation.1 | async-start | bytes 2621440 | tf_op jit(solution)/shard_map/all_to_all | solution.py:132
  231.1 31.7 %all-to-all-done.1 = bf16[64,3,2560]{2,1,0:T(4,128)(2,1)S(1)} async-done(((bf16[64,3,2560]{2,1,0:T(4,128)(2,1)}), bf16[64,3,2560]{2,1,0:T(4,128)(2,1)S(1)}, u32[]{:S(2)}, u32[]{:S(2)}) %all-to-all-start.1) | async-done | bytes 983072 | tf_op jit(solution)/shard_map/all_to_all | solution.py:132
  262.8 1.0 broadcast_in_dim.8
  263.8 3.5 %all-to-all-start.4 = ((f32[8,48,416]{2,1,0:T(8,128)}), f32[8,48,416]{2,1,0:T(8,128)S(1)}, u32[]{:S(2)}, u32[]{:S(2)}) async-start(f32[8,48,416]{2,1,0:T(8,128)} %broadcast_in_dim.8), calls=%async_computation.5 | async-start | bytes 1572864 | tf_op jit(solution)/shard_map/all_to_all | solution.py:123
  267.4 0.2 copy.157
  267.7 1.0 copy.104
  268.7 1.0 copy.105
  269.7 19.1 %all-to-all-done.4 = f32[8,48,416]{2,1,0:T(8,128)S(1)} async-done(((f32[8,48,416]{2,1,0:T(8,128)}), f32[8,48,416]{2,1,0:T(8,128)S(1)}, u32[]{:S(2)}, u32[]{:S(2)}) %all-to-all-start.4) | async-done | bytes 639008 | tf_op jit(solution)/shard_map/all_to_all | solution.py:123
  288.8 0.9 copy.116
  289.7 0.7 reshape_squeeze.7
  (49 shorter events, 0.9 us)
Async XLA Ops:
  7.2 2.0 copy-start.6
  7.2 66.5 %all-gather.2.cloned.1.call-start = ((), (), s32[]{:S(2)}) async-start(), calls=%async_computation.6 | async-start | bytes 9732096 | tf_op jit(solution)/shard_map/all_gather | solution.py:61
  7.9 189.3 %reduce-scatter.2.cloned.1.call-start = ((), (), s32[]{:S(2)}) async-start(), calls=%async_computation.7 | async-start | bytes 7299072 | tf_op jit(solution)/shard_map/reduce_scatter | solution.py:96
  45.5 1.0 copy-start
  46.6 27.1 %copy-start.14 = (f32[1536]{0:T(1024)S(1)}, f32[1536]{0:T(1024)}, u32[]{:S(2)}) copy-start(f32[1536]{0:T(1024)} %param.5) | copy-start | bytes 18436
  46.7 32.6 %copy-start.3 = (f32[192,1536]{1,0:T(8,128)}, f32[192,1536]{1,0:T(8,128)S(1)}, u32[]{:S(2)}) copy-start(f32[192,1536]{1,0:T(8,128)S(1)} %bitcast_multiply_fusion) | copy-start | bytes 3538948
  80.5 1.7 copy-start.7
  85.4 1.0 copy-start.10
  86.4 1.1 copy-start.9
  86.4 1.3 copy-start.8
  89.3 1.3 copy-start.11
  90.3 1.4 copy-start.4
  90.7 1.0 copy-start.12
  94.9 3.7 %copy-start.2 = (bf16[1536,3072]{1,0:T(8,128)(2,1)}, bf16[1536,3072]{1,0:T(8,128)(2,1)S(1)}, u32[]{:S(2)}) copy-start(bf16[1536,3072]{1,0:T(8,128)(2,1)S(1)} %multiply_convert_fusion) | copy-start | bytes 28311556
  102.1 1.3 copy-start.5
  102.1 1.6 copy-start.13
  103.7 8.9 %slice-start = ((bf16[1536,3072]{1,0:T(8,128)(2,1)}), bf16[1536,768]{1,0:T(8,128)(2,1)S(1)}, s32[]{:S(2)}) async-start(bf16[1536,3072]{1,0:T(8,128)(2,1)} %copy-done.2), calls=%async_computation.8 | async-start | bytes 4718592 | tf_op jit(solution)/shard_map/slice | solution.py:105
  114.5 41.2 %all-to-all-start.2 = ((bf16[32,48,832]{2,1,0:T(8,128)(2,1)}), bf16[32,48,832]{2,1,0:T(8,128)(2,1)S(1)}, u32[]{:S(2)}, u32[]{:S(2)}) async-start(bf16[32,48,832]{2,1,0:T(8,128)(2,1)} %pad_maximum_fusion), calls=%async_computation.3 | async-start | bytes 5505024 | tf_op jit(solution)/shard_map/all_to_all | solution.py:111
  155.7 0.7 copy-start.15
  199.3 7.1 %copy-start.1 = (f32[3,64,1536]{2,1,0:T(8,128)S(1)}, f32[3,64,1536]{2,1,0:T(8,128)}, u32[]{:S(2)}) copy-start(f32[3,64,1536]{2,1,0:T(8,128)} %copy-done) | copy-start | bytes 3538948
  199.3 28.1 %all-to-all-start.3 = ((f32[8,48,416]{2,1,0:T(8,128)}), f32[8,48,416]{2,1,0:T(8,128)S(1)}, u32[]{:S(2)}, u32[]{:S(2)}) async-start(f32[8,48,416]{2,1,0:T(8,128)} %pad_maximum_fusion.2), calls=%async_computation.4 | async-start | bytes 1572864 | tf_op jit(solution)/shard_map/all_to_all | solution.py:120
  227.5 35.3 %all-to-all-start.1 = ((bf16[64,3,2560]{2,1,0:T(4,128)(2,1)}), bf16[64,3,2560]{2,1,0:T(4,128)(2,1)S(1)}, u32[]{:S(2)}, u32[]{:S(2)}) async-start(bf16[64,3,2560]{2,1,0:T(4,128)(2,1)} %maximum_bitcast_fusion), calls=%async_computation.1 | async-start | bytes 2621440 | tf_op jit(solution)/shard_map/all_to_all | solution.py:132
  263.8 25.0 %all-to-all-start.4 = ((f32[8,48,416]{2,1,0:T(8,128)}), f32[8,48,416]{2,1,0:T(8,128)S(1)}, u32[]{:S(2)}, u32[]{:S(2)}) async-start(f32[8,48,416]{2,1,0:T(8,128)} %broadcast_in_dim.8), calls=%async_computation.5 | async-start | bytes 1572864 | tf_op jit(solution)/shard_map/all_to_all | solution.py:123
Sparse Core Ops, SparseCore 0:
  10.5 63.0 all-gather.1
  102.2 94.9 reduce-scatter.1

commit v5 on v1

--- a/solution.py
+++ b/solution.py
@@ -4,6 +4,7 @@
 import jax.numpy as jnp
 from jax import lax
 from jax.sharding import PartitionSpec as P
+
 
 HEADS = 8
 HDIM = 128
@@ -45,7 +46,7 @@
     return attended, query_grad, key_grad, value_grad
 
 
-def per_device(tokens, norm_gain, qkv_weight, out_grad):
+def per_device_body(tokens, norm_gain, qkv_weight, out_grad):
     joint_rows, frame_rows, width = tokens.shape
     inner = out_grad.shape[2]
     joint_count = lax.axis_size("joint")
@@ -89,8 +90,14 @@
     frame_sum = lax.psum_scatter(
         (product * grad_scale).astype(jnp.bfloat16), "frame", scatter_dimension=0, tiled=True
     )
-    joint_part = lax.psum_scatter(frame_sum, "joint", scatter_dimension=1, tiled=True)
-    weight_grad = lax.all_gather(joint_part, "joint", axis=1, tiled=True).astype(jnp.float32)
+    row_count = frame_sum.shape[0]
+    col_block = 3 * inner // joint_count
+    blocks = frame_sum.reshape(row_count, joint_count, col_block).transpose(1, 0, 2)
+    blocks = lax.all_to_all(blocks, "joint", 0, 0, tiled=True)
+    block_sum = jnp.sum(blocks.astype(jnp.float32), axis=0)
+    spread = jnp.broadcast_to(block_sum.astype(jnp.bfloat16)[None], (joint_count, row_count, col_block))
+    spread = lax.all_to_all(spread, "joint", 0, 0, tiled=True)
+    weight_grad = spread.transpose(1, 0, 2).reshape(row_count, 3 * inner).astype(jnp.float32)
     normed_grad = lax.dot_general(
         qkv_grad, whole, (((1,), (1,)), ((), ())), preferred_element_type=jnp.float32
     )
@@ -111,7 +118,7 @@
 def solution(mesh):
     placed = (P("joint", "frame", None), P(), P("frame", None), P("joint", "frame", None))
     return jax.shard_map(
-        per_device,
+        per_device_body,
         mesh=mesh,
         in_specs=placed,
         out_specs=(P("joint", "frame", None), P("joint", "frame", None), P("frame", None), P()),

time: 319 us -> 348 us (1.091)
  waiting for transfers between devices: 113 us -> 162 us
  blocking collectives: 134 us -> 109 us
  starting transfers between devices: 7.13 us -> 14 us
    all_to_all x1 -> x3, waiting for transfers between devices: 0.01 us -> 39.5 us  [the longest x1 31.4 us: per_device_body(): back = lax.all_to_all(back, 'joint', 0, 1, tiled=True)]
    all_gather x1 -> x0, blocking collectives: 25.1 us -> none  [per_device(): lax.all_gather(joint_part, 'joint', axis=1, tiled=True).astype(jnp.float32)]
    reduce_scatter x1, waiting for transfers between devices: 84.1 us -> 94.9 us  [per_device_body(): lax.psum_scatter((product * grad_scale).astype(jnp.bfloat16), 'frame', sc...]
    all_to_all x1 -> x3, starting transfers between devices: 7.01 us -> 14 us  [the longest x1 6.98 us: per_device_body(): blocks = lax.all_to_all(blocks, 'joint', 0, 0, tiled=True)]
    unnamed x29 -> x23, local copies, waits for them, and re-layouts: 9.18 us -> 5.15 us
  transfers between devices with their start and end apart: 4 -> 5, of which waited for: 2 -> 4; matrix products, arithmetic and copies ran while one was open for 5% -> 5% of each run, Pallas kernels for 0% -> 0%
where the time goes in v5:
time: 348 us; the launch traced here: 345 us
  waiting for transfers between devices  162 us (47%)
  blocking collectives  109 us (31%)
  matrix products  26.5 us (8%)
  between operations  14.4 us (4%)
  starting transfers between devices  14 us (4%)
  local copies, waits for them, and re-layouts  12.3 us (4%)
  other arithmetic  6.59 us (2%)
    reduce_scatter x1, waiting for transfers between devices, per_device_body(): lax.psum_scatter((product * grad_scale).astype(jnp.bfloat16), 'frame', sc...  94.9 us
    psum x1, blocking collectives, per_device_body(): gain_grad = lax.psum(gain_part, ('joint', 'frame'))  73.4 us
    all_to_all x1, blocking collectives, per_device_body(): packed = lax.all_to_all(packed, 'joint', 1, 0, tiled=True)  35.6 us
    all_to_all x1, waiting for transfers between devices, per_device_body(): back = lax.all_to_all(back, 'joint', 0, 1, tiled=True)  31.4 us
    all_gather x1, waiting for transfers between devices, per_device_body(): whole = lax.all_gather(qkv_weight, 'frame', axis=0, tiled=True)  26.9 us
    all_to_all x1, waiting for transfers between devices, per_device_body(): blocks = lax.all_to_all(blocks, 'joint', 0, 0, tiled=True)  8.01 us
    dot_general x1, matrix products, per_device_body(): lax.dot_general(qkv_grad, whole, (((1,), (1,)), ((), ())), preferred_elem...  7.46 us
    all_to_all x1, starting transfers between devices, per_device_body(): blocks = lax.all_to_all(blocks, 'joint', 0, 0, tiled=True)  6.98 us
  transfers between devices with their start and end apart: 5, of which 4 were waited for; matrix products, arithmetic and copies ran while one was open for 5% of the time, Pallas kernels for 0%

profile of v5, /device:TPU:2, one launch (start us, length us, event | category | flops | bytes accessed | tf_op | source)
XLA Modules:
  0.0 344.8 jit_solution(9512950270879708766)
XLA Ops:
  7.2 0.0 copy-start.2
  7.2 0.0 all-gather.2.cloned.1.call-start
  7.2 0.7 all-gather.2.cloned.1.call-update
  7.9 0.0 reduce-scatter.2.cloned.1.call-start
  8.0 1.2 copy.78
  9.2 0.0 copy-done.2
  9.2 0.2 copy.77
  9.4 0.1 pad_maximum_fusion
  9.4 35.6 %all_to_all.46 = bf16[8,24,2560]{2,0,1:T(8,128)(2,1)S(1)} all-to-all(bf16[8,24,2560]{2,0,1:T(8,128)(2,1)S(1)} %pad_maximum_fusion), channel_id=1, replica_groups=mesh['joint'=8,'frame'=32] {'joint'}, dimensions={1} | all-to-all | bytes 1966080 | tf_op jit(solution)/shard_map/all_to_all | solution.py:63
  45.0 0.1 copy.155
  45.1 0.2 multiply_reduce_fusion.2
  45.3 0.1 rsqrt.12
  45.4 0.1 slice_convert_fusion
  45.5 0.0 copy-start.7
  45.6 1.1 bitcast_multiply_fusion
  46.7 26.9 %all-gather.2.cloned.1.call-done = bf16[1536,3072]{1,0:T(8,128)(2,1)} async-done(((bf16[48,3072]{1,0:T(8,128)(2,1)}), bf16[1536,3072]{1,0:T(8,128)(2,1)}) %all-gather.2.cloned.1.call-update) | async-done | bytes 9437200 | tf_op jit(solution)/shard_map/all_gather | solution.py:60
  73.6 0.0 copy-done.7
  73.6 6.1 %fusion.3 = bf16[24,8,24,128]{3,1,2,0:T(8,128)(2,1)S(1)} fusion(bf16[1536,3072]{1,0:T(8,128)(2,1)} %all-gather.2.cloned.1.call-done, f32[192,1536]{1,0:T(8,128)} %bitcast_multiply_fusion, f32[1536]{0:T(1024)S(1)} %copy-done.7), kind=kOutput, calls=%fused_computation.7 | convolution fusion | flops 1813118976 | bytes 11802624 | tf_op jit(solution)/shard_map/dot_general | solution.py:71
  79.7 0.2 copy.114
  79.9 0.2 fusion.27
  80.2 0.0 copy-start.3
  80.2 1.2 fusion.12
  81.4 1.3 fusion.28
  82.7 3.0 fusion.10
  85.7 2.9 fusion.8
  88.6 0.1 fusion.26
  88.7 0.2 copy.92
  88.9 1.0 convert_reduce_fusion
  90.0 0.0 copy-start.4
  90.0 0.3 copy.94
  90.3 1.2 copy.88
  91.5 0.0 copy-start.5
  91.5 1.0 convert_reduce_fusion.1
  92.5 0.3 copy.91
  92.8 0.3 copy.87
  93.1 0.1 bitcast_dynamic-update-slice_fusion.2
  93.1 0.1 bitcast_dynamic-update-slice_fusion.1
  93.2 0.1 bitcast_dynamic-update-slice_fusion
  93.3 1.0 copy-done.6
  94.3 0.4 copy-done
  94.7 5.1 %multiply_convert_fusion = bf16[1536,3072]{1,0:T(8,128)(2,1)} fusion(bf16[192,3072]{1,0:T(8,128)(2,1)S(1)} %bitcast_dynamic-update-slice_fusion, f32[192,1536]{1,0:T(8,128)S(1)} %copy-done, f32[1536]{0:T(1024)S(1)} %copy-done.7), kind=kOutput, calls=%fused_computation.2 | convolution fusion | flops 1821966336 | bytes 11802624 | tf_op jit(solution)/shard_map/dot_general | solution.py:87
  99.8 0.0 reduce-scatter.2.cloned.1.call-update
  99.8 7.5 %multiply_reduce_fusion = (f32[1536]{0:T(1024)S(1)}, f32[192]{0:T(256)S(1)}, f32[192,1536]{1,0:T(8,128)S(1)}) fusion(f32[192,1536]{1,0:T(8,128)S(1)} %copy-done, f32[1536]{0:T(1024)S(1)} %copy-done.7, bf16[192,3072]{1,0:T(8,128)(2,1)} %copy-done.6, bf16[1536,3072]{1,0:T(8,128)(2,1)} %all-gather.2.cloned.1.call-done), kind=kOutput, calls=%fused_computation.20 | convolution fusion | flops 1813412096 | bytes 12989184 | tf_op jit(solution)/shard_map/dot_general | solution.py:101
  107.3 0.3 multiply_convert_fusion.1
  107.6 94.9 %reduce-scatter.2.cloned.1.call-done = bf16[48,3072]{1,0:T(8,128)(2,1)} async-done(((bf16[1536,3072]{1,0:T(8,128)(2,1)}), bf16[48,3072]{1,0:T(8,128)(2,1)}) %reduce-scatter.2.cloned.1.call-update) | async-done | bytes 294928 | tf_op jit(solution)/shard_map/reduce_scatter | solution.py:90
  202.5 1.7 copy.156
  204.2 7.0 %all-to-all-start.2 = ((bf16[8,48,384]{2,1,0:T(8,128)(2,1)}), bf16[8,48,384]{2,1,0:T(8,128)(2,1)S(1)}, u32[]{:S(2)}, u32[]{:S(2)}) async-start(bf16[8,48,384]{2,1,0:T(8,128)(2,1)} %bitcast.105), calls=%async_computation.3 | async-start | bytes 589824 | tf_op jit(solution)/shard_map/all_to_all | solution.py:96
  211.2 0.3 fusion.9
  211.5 0.3 copy.105
  211.8 0.1 reshape.82
  211.9 0.5 copy.96
  212.4 1.7 maximum_bitcast_fusion
  214.0 8.0 %all-to-all-done.2 = bf16[8,48,384]{2,1,0:T(8,128)(2,1)S(1)} async-done(((bf16[8,48,384]{2,1,0:T(8,128)(2,1)}), bf16[8,48,384]{2,1,0:T(8,128)(2,1)S(1)}, u32[]{:S(2)}, u32[]{:S(2)}) %all-to-all-start.2) | async-done | bytes 294944 | tf_op jit(solution)/shard_map/all_to_all | solution.py:96
  222.1 3.6 %all-to-all-start.1 = ((bf16[64,3,2560]{2,1,0:T(4,128)(2,1)}), bf16[64,3,2560]{2,1,0:T(4,128)(2,1)S(1)}, u32[]{:S(2)}, u32[]{:S(2)}) async-start(bf16[64,3,2560]{2,1,0:T(4,128)(2,1)} %maximum_bitcast_fusion), calls=%async_computation.1 | async-start | bytes 2621440 | tf_op jit(solution)/shard_map/all_to_all | solution.py:112
  225.7 31.4 %all-to-all-done.1 = bf16[64,3,2560]{2,1,0:T(4,128)(2,1)S(1)} async-done(((bf16[64,3,2560]{2,1,0:T(4,128)(2,1)}), bf16[64,3,2560]{2,1,0:T(4,128)(2,1)S(1)}, u32[]{:S(2)}, u32[]{:S(2)}) %all-to-all-start.1) | async-done | bytes 983072 | tf_op jit(solution)/shard_map/all_to_all | solution.py:112
  257.1 0.7 broadcast_in_dim.2
  257.9 3.4 all-to-all-start.3
  261.3 73.4 %psum.7 = f32[1536]{0:T(1024)} all-reduce(f32[1536]{0:T(1024)S(1)} %broadcast_multiply_fusion), channel_id=1, replica_groups=mesh['joint'=8,'frame'=32] {'joint','frame'}, use_global_device_ids=true, to_apply=%region_10.0 | all-reduce | flops 1536 | bytes 12288 | tf_op jit(solution)/shard_map/psum | solution.py:105
  334.7 0.2 copy.154
  334.9 0.1 copy.98
  335.1 1.0 copy.102
  336.1 1.0 copy.101
  337.1 0.0 all-to-all-done.3
  337.1 0.9 copy.113
  (14 shorter events, 0.2 us)
Async XLA Ops:
  7.2 2.0 copy-start.2
  7.2 66.5 %all-gather.2.cloned.1.call-start = ((), (), s32[]{:S(2)}) async-start(), calls=%async_computation.5 | async-start | bytes 9732096 | tf_op jit(solution)/shard_map/all_gather | solution.py:60
  7.9 194.6 %reduce-scatter.2.cloned.1.call-start = ((), (), s32[]{:S(2)}) async-start(), calls=%async_computation.6 | async-start | bytes 9732096 | tf_op jit(solution)/shard_map/reduce_scatter | solution.py:90
  45.5 28.1 %copy-start.7 = (f32[1536]{0:T(1024)S(1)}, f32[1536]{0:T(1024)}, u32[]{:S(2)}) copy-start(f32[1536]{0:T(1024)} %param.5) | copy-start | bytes 18436
  80.2 2.5 copy-start.3
  85.7 2.9 copy-start.1
  90.0 1.5 copy-start.4
  91.5 1.3 copy-start.5
  93.1 1.7 copy-start
  93.3 1.0 copy-start.6
  204.2 17.8 %all-to-all-start.2 = ((bf16[8,48,384]{2,1,0:T(8,128)(2,1)}), bf16[8,48,384]{2,1,0:T(8,128)(2,1)S(1)}, u32[]{:S(2)}, u32[]{:S(2)}) async-start(bf16[8,48,384]{2,1,0:T(8,128)(2,1)} %bitcast.105), calls=%async_computation.3 | async-start | bytes 589824 | tf_op jit(solution)/shard_map/all_to_all | solution.py:96
  222.1 35.1 %all-to-all-start.1 = ((bf16[64,3,2560]{2,1,0:T(4,128)(2,1)}), bf16[64,3,2560]{2,1,0:T(4,128)(2,1)S(1)}, u32[]{:S(2)}, u32[]{:S(2)}) async-start(bf16[64,3,2560]{2,1,0:T(4,128)(2,1)} %maximum_bitcast_fusion), calls=%async_computation.1 | async-start | bytes 2621440 | tf_op jit(solution)/shard_map/all_to_all | solution.py:112
  257.9 79.2 %all-to-all-start.3 = ((bf16[8,48,384]{2,1,0:T(8,128)(2,1)}), bf16[8,48,384]{2,1,0:T(8,128)(2,1)S(1)}, u32[]{:S(2)}, u32[]{:S(2)}) async-start(bf16[8,48,384]{2,1,0:T(8,128)(2,1)} %broadcast_in_dim.2), calls=%async_computation.4 | async-start | bytes 589824 | tf_op jit(solution)/shard_map/all_to_all | solution.py:99
Sparse Core Ops, SparseCore 0:
  10.5 63.0 all-gather.1
  100.0 102.4 reduce-scatter.1

commit v6 on v5

--- a/solution.py
+++ b/solution.py
@@ -84,12 +84,18 @@
         ],
         axis=1,
     )
+    value_product = lax.dot_general(
+        scaled, value_grad.reshape(count, inner), (((0,), (0,)), ((), ())),
+        preferred_element_type=jnp.float32,
+    )
+    value_sum = lax.psum_scatter(
+        (value_product * grad_scale).astype(jnp.bfloat16), "frame", scatter_dimension=0, tiled=True
+    )
     product = lax.dot_general(
-        scaled, qkv_grad, (((0,), (0,)), ((), ())), preferred_element_type=jnp.float32
+        scaled, qkv_grad[:, : 2 * inner], (((0,), (0,)), ((), ())), preferred_element_type=jnp.float32
     )
-    frame_sum = lax.psum_scatter(
-        (product * grad_scale).astype(jnp.bfloat16), "frame", scatter_dimension=0, tiled=True
-    )
+    frame_sum = lax.psum_scatter((product * grad_scale).astype(jnp.bfloat16), "frame", scatter_dimension=0, tiled=True)
+    frame_sum = jnp.concatenate([frame_sum, value_sum], axis=1)
     row_count = frame_sum.shape[0]
     col_block = 3 * inner // joint_count
     blocks = frame_sum.reshape(row_count, joint_count, col_block).transpose(1, 0, 2)

time: 348 us -> 419 us (1.20)
  waiting for transfers between devices: 162 us -> 228 us
    reduce_scatter x0 -> x1, waiting for transfers between devices: none -> 65.9 us  [per_device_body(): lax.psum_scatter((value_product * grad_scale).astype(jnp.bfloat16), 'fram...]
  transfers between devices with their start and end apart: 5 -> 6, of which waited for: 4 -> 5; matrix products, arithmetic and copies ran while one was open for 5% -> 7% of each run, Pallas kernels for 0% -> 0%
where the time goes in v6:
time: 419 us; the launch traced here: 416 us
  waiting for transfers between devices  228 us (54%)
  blocking collectives  110 us (26%)
  matrix products  28.8 us (7%)
  starting transfers between devices  14.3 us (3%)
  between operations  14.1 us (3%)
  local copies, waits for them, and re-layouts  13.5 us (3%)
  other arithmetic  7.07 us (2%)
    reduce_scatter x1, waiting for transfers between devices, per_device_body(): lax.psum_scatter((product * grad_scale).astype(jnp.bfloat16), 'frame', sc...  97.3 us
    psum x1, blocking collectives, per_device_body(): gain_grad = lax.psum(gain_part, ('joint', 'frame'))  74 us
    reduce_scatter x1, waiting for transfers between devices, per_device_body(): lax.psum_scatter((value_product * grad_scale).astype(jnp.bfloat16), 'fram...  65.9 us
    all_to_all x1, blocking collectives, per_device_body(): packed = lax.all_to_all(packed, 'joint', 1, 0, tiled=True)  35.6 us
    all_to_all x1, waiting for transfers between devices, per_device_body(): back = lax.all_to_all(back, 'joint', 0, 1, tiled=True)  30.9 us
    all_gather x1, waiting for transfers between devices, per_device_body(): whole = lax.all_gather(qkv_weight, 'frame', axis=0, tiled=True)  25.6 us
  transfers between devices with their start and end apart: 6, of which 5 were waited for; matrix products, arithmetic and copies ran while one was open for 7% of the time, Pallas kernels for 0%

profile of v6, /device:TPU:2, one launch (start us, length us, event | category | flops | bytes accessed | tf_op | source)
XLA Modules:
  0.0 415.8 jit_solution(8941515604976779286)
XLA Ops:
  7.2 0.0 all-gather.2.cloned.1.call-start
  7.2 0.7 all-gather.2.cloned.1.call-update
  7.9 0.0 reduce-scatter.5.cloned.1.call-start
  8.0 1.2 copy.78
  9.2 0.2 copy.77
  9.4 0.1 pad_maximum_fusion
  9.4 35.6 %all_to_all.46 = bf16[8,24,2560]{2,0,1:T(8,128)(2,1)S(1)} all-to-all(bf16[8,24,2560]{2,0,1:T(8,128)(2,1)S(1)} %pad_maximum_fusion), channel_id=1, replica_groups=mesh['joint'=8,'frame'=32] {'joint'}, dimensions={1} | all-to-all | bytes 1966080 | tf_op jit(solution)/shard_map/all_to_all | solution.py:63
  45.0 0.1 copy.156
  45.1 0.2 multiply_reduce_fusion.2
  45.3 0.1 rsqrt.13
  45.4 0.3 copy-done.12
  45.7 1.0 multiply_convert_fusion.2
  46.7 0.1 slice_convert_fusion
  46.9 1.2 bitcast_multiply_fusion
  48.1 25.6 %all-gather.2.cloned.1.call-done = bf16[1536,3072]{1,0:T(8,128)(2,1)} async-done(((bf16[48,3072]{1,0:T(8,128)(2,1)}), bf16[1536,3072]{1,0:T(8,128)(2,1)}) %all-gather.2.cloned.1.call-update) | async-done | bytes 9437200 | tf_op jit(solution)/shard_map/all_gather | solution.py:60
  73.6 6.1 %fusion.3 = bf16[24,8,24,128]{3,1,2,0:T(8,128)(2,1)S(1)} fusion(bf16[1536,3072]{1,0:T(8,128)(2,1)} %all-gather.2.cloned.1.call-done, f32[192,1536]{1,0:T(8,128)} %bitcast_multiply_fusion, f32[1536]{0:T(1024)S(1)} %copy-done.12), kind=kOutput, calls=%fused_computation.8 | convolution fusion | flops 1813118976 | bytes 11802624 | tf_op jit(solution)/shard_map/dot_general | solution.py:71
  79.7 0.2 copy.114
  79.9 0.2 fusion.38
  80.2 1.3 fusion.39
  81.5 1.2 fusion.37
  82.7 0.9 copy.92
  83.7 2.1 convert_reduce_fusion
  85.8 0.3 copy.94
  86.1 2.7 multiply_convert_fusion.1
  88.7 0.0 reduce-scatter.5.cloned.1.call-update
  88.8 0.2 reduce-scatter.3.cloned.1.call-start
  89.0 0.3 fusion.21
  89.3 0.9 copy-done.3
  90.3 0.2 fusion.8
  90.5 0.2 copy.88
  90.7 0.5 copy-done.9
  91.3 1.0 convert_reduce_fusion.1
  92.3 0.3 copy.91
  92.6 2.3 fusion.10
  94.9 0.3 copy.87
  95.2 0.1 copy_bitcast_fusion.3
  95.3 0.7 copy-done.10
  96.0 0.1 copy-done.11
  96.2 4.5 %multiply_convert_fusion = bf16[1536,2048]{1,0:T(8,128)(2,1)} fusion(bf16[192,1024]{1,0:T(8,128)(2,1)S(1)} %get-tuple-element.28, bf16[192,1024]{1,0:T(8,128)(2,1)S(1)} %get-tuple-element.29, f32[192,1536]{1,0:T(8,128)S(1)} %copy-done, f32[1536]{0:T(1024)S(1)} %copy-done.12), kind=kOutput, calls=%fused_computation.2 | convolution fusion | flops 1216413696 | bytes 8263680 | tf_op jit(solution)/shard_map/dot_general | solution.py:94
  100.7 0.1 copy.157
  100.8 1.2 copy-done.1
  102.0 8.2 %multiply_reduce_fusion = (f32[1536]{0:T(1024)}, f32[192]{0:T(256)S(1)}, f32[192,1536]{1,0:T(8,128)S(1)}) fusion(f32[192,1536]{1,0:T(8,128)S(1)} %copy-done.1, f32[1536]{0:T(1024)S(1)} %copy-done.12, bf16[1536,3072]{1,0:T(8,128)(2,1)} %all-gather.2.cloned.1.call-done, bf16[192,1024]{1,0:T(8,128)(2,1)S(1)} %bitcast.127, bf16[192,1024]{1,0:T(8,128)(2,1)} %copy-done.10, ...), kind=kOutput, calls=%fused_computation.27 | convolution fusion | flops 1816951040 | bytes 12989184 | tf_op jit(solution)/shard_map/dot_general | solution.py:107
  110.1 0.3 multiply_convert_fusion.3
  110.4 65.9 %reduce-scatter.5.cloned.1.call-done = bf16[48,1024]{1,0:T(8,128)(2,1)} async-done(((bf16[1536,1024]{1,0:T(8,128)(2,1)}), bf16[48,1024]{1,0:T(8,128)(2,1)}) %reduce-scatter.5.cloned.1.call-update) | async-done | bytes 98320 | tf_op jit(solution)/shard_map/reduce_scatter | solution.py:91
  176.3 97.3 %reduce-scatter.3.cloned.1.call-done = bf16[48,2048]{1,0:T(8,128)(2,1)} async-done(((bf16[1536,2048]{1,0:T(8,128)(2,1)}), bf16[48,2048]{1,0:T(8,128)(2,1)}) %reduce-scatter.3.cloned.1.call-update) | async-done | bytes 196624 | tf_op jit(solution)/shard_map/reduce_scatter | solution.py:97
  273.7 1.0 pad_maximum_fusion.1
  274.7 0.7 copy.158
  275.4 7.0 %all-to-all-start.2 = ((bf16[8,48,384]{2,1,0:T(8,128)(2,1)}), bf16[8,48,384]{2,1,0:T(8,128)(2,1)S(1)}, u32[]{:S(2)}, u32[]{:S(2)}) async-start(bf16[8,48,384]{2,1,0:T(8,128)(2,1)} %bitcast.107), calls=%async_computation.4 | async-start | bytes 589824 | tf_op jit(solution)/shard_map/all_to_all | solution.py:102
  282.4 0.3 fusion.9
  282.7 0.3 copy.105
  283.0 0.1 reshape.93
  283.1 0.5 copy.96
  283.6 1.7 maximum_bitcast_fusion
  285.3 8.0 %all-to-all-done.2 = bf16[8,48,384]{2,1,0:T(8,128)(2,1)S(1)} async-done(((bf16[8,48,384]{2,1,0:T(8,128)(2,1)}), bf16[8,48,384]{2,1,0:T(8,128)(2,1)S(1)}, u32[]{:S(2)}, u32[]{:S(2)}) %all-to-all-start.2) | async-done | bytes 294944 | tf_op jit(solution)/shard_map/all_to_all | solution.py:102
  293.2 3.6 all-to-all-start.1
  296.9 30.9 %all-to-all-done.1 = bf16[64,3,2560]{2,1,0:T(4,128)(2,1)S(1)} async-done(((bf16[64,3,2560]{2,1,0:T(4,128)(2,1)}), bf16[64,3,2560]{2,1,0:T(4,128)(2,1)S(1)}, u32[]{:S(2)}, u32[]{:S(2)}) %all-to-all-start.1) | async-done | bytes 983072 | tf_op jit(solution)/shard_map/all_to_all | solution.py:118
  327.8 0.7 broadcast_in_dim.2
  328.6 3.4 all-to-all-start.3
  332.0 74.0 %psum.7 = f32[1536]{0:T(1024)} all-reduce(f32[1536]{0:T(1024)S(1)} %broadcast_multiply_fusion), channel_id=1, replica_groups=mesh['joint'=8,'frame'=32] {'joint','frame'}, use_global_device_ids=true, to_apply=%region_11.0 | all-reduce | flops 1536 | bytes 12288 | tf_op jit(solution)/shard_map/psum | solution.py:111
  406.1 0.2 copy.155
  406.3 0.1 copy.98
  406.4 1.0 copy.102
  407.4 1.0 copy.101
  408.4 0.9 copy.113
  (33 shorter events, 0.3 us)
Async XLA Ops:
  7.2 2.0 copy-start.4
  7.2 66.5 %all-gather.2.cloned.1.call-start = ((), (), s32[]{:S(2)}) async-start(), calls=%async_computation.6 | async-start | bytes 9732096 | tf_op jit(solution)/shard_map/all_gather | solution.py:60
  7.9 168.4 %reduce-scatter.5.cloned.1.call-start = ((), (), s32[]{:S(2)}) async-start(), calls=%async_computation.8 | async-start | bytes 3244032 | tf_op jit(solution)/shard_map/reduce_scatter | solution.py:91
  45.0 0.7 copy-start.12
  80.2 1.3 copy-start.6
  80.2 2.5 copy-start.8
  81.5 7.9 %copy-start.13 = (f32[3,8,64]{2,1,0:T(8,128)}, f32[3,8,64]{2,1,0:T(8,128)S(1)}, u32[]{:S(2)}) copy-start(f32[3,8,64]{2,1,0:T(8,128)S(1)} %get-tuple-element.25) | copy-start | bytes 18436
  83.6 2.4 copy-start.5
  88.8 184.9 %reduce-scatter.3.cloned.1.call-start = ((), (), s32[]{:S(2)}) async-start(), calls=%async_computation.7 | async-start | bytes 6488064 | tf_op jit(solution)/shard_map/reduce_scatter | solution.py:97
  89.0 1.3 copy-start.2
  89.3 0.9 copy-start.3
  90.3 1.0 copy-start.9
  91.3 1.3 copy-start.7
  94.9 1.3 copy-start
  95.3 0.7 copy-start.10
  95.3 0.9 copy-start.11
  100.7 1.3 copy-start.1
  275.4 17.9 %all-to-all-start.2 = ((bf16[8,48,384]{2,1,0:T(8,128)(2,1)}), bf16[8,48,384]{2,1,0:T(8,128)(2,1)S(1)}, u32[]{:S(2)}, u32[]{:S(2)}) async-start(bf16[8,48,384]{2,1,0:T(8,128)(2,1)} %bitcast.107), calls=%async_computation.4 | async-start | bytes 589824 | tf_op jit(solution)/shard_map/all_to_all | solution.py:102
  293.2 34.6 %all-to-all-start.1 = ((bf16[64,3,2560]{2,1,0:T(4,128)(2,1)}), bf16[64,3,2560]{2,1,0:T(4,128)(2,1)S(1)}, u32[]{:S(2)}, u32[]{:S(2)}) async-start(bf16[64,3,2560]{2,1,0:T(4,128)(2,1)} %maximum_bitcast_fusion), calls=%async_computation.1 | async-start | bytes 2621440 | tf_op jit(solution)/shard_map/all_to_all | solution.py:118
  296.8 35.2 %copy-start.14 = (f32[1536]{0:T(1024)S(1)}, f32[1536]{0:T(1024)}, u32[]{:S(2)}) copy-start(f32[1536]{0:T(1024)} %get-tuple-element.20) | copy-start | bytes 18436
  328.6 79.8 %all-to-all-start.3 = ((bf16[8,48,384]{2,1,0:T(8,128)(2,1)}), bf16[8,48,384]{2,1,0:T(8,128)(2,1)S(1)}, u32[]{:S(2)}, u32[]{:S(2)}) async-start(bf16[8,48,384]{2,1,0:T(8,128)(2,1)} %broadcast_in_dim.2), calls=%async_computation.5 | async-start | bytes 589824 | tf_op jit(solution)/shard_map/all_to_all | solution.py:105
Sparse Core Ops, SparseCore 0:
  10.5 63.0 all-gather.1
  88.9 87.4 reduce-scatter.4
  180.4 93.2 reduce-scatter.2

commit v7 on v1

--- a/solution.py
+++ b/solution.py
@@ -4,6 +4,7 @@
 import jax.numpy as jnp
 from jax import lax
 from jax.sharding import PartitionSpec as P
+
 
 HEADS = 8
 HDIM = 128
@@ -45,7 +46,7 @@
     return attended, query_grad, key_grad, value_grad
 
 
-def per_device(tokens, norm_gain, qkv_weight, out_grad):
+def per_device_body(tokens, norm_gain, qkv_weight, out_grad):
     joint_rows, frame_rows, width = tokens.shape
     inner = out_grad.shape[2]
     joint_count = lax.axis_size("joint")
@@ -89,8 +90,14 @@
     frame_sum = lax.psum_scatter(
         (product * grad_scale).astype(jnp.bfloat16), "frame", scatter_dimension=0, tiled=True
     )
-    joint_part = lax.psum_scatter(frame_sum, "joint", scatter_dimension=1, tiled=True)
-    weight_grad = lax.all_gather(joint_part, "joint", axis=1, tiled=True).astype(jnp.float32)
+    weight_grad = frame_sum
+    step = 1
+    while step < joint_count:
+        pairs = [(j, j ^ step) for j in range(joint_count)]
+        other = lax.ppermute(weight_grad, "joint", pairs)
+        weight_grad = (weight_grad.astype(jnp.float32) + other.astype(jnp.float32)).astype(jnp.bfloat16)
+        step *= 2
+    weight_grad = weight_grad.astype(jnp.float32)
     normed_grad = lax.dot_general(
         qkv_grad, whole, (((1,), (1,)), ((), ())), preferred_element_type=jnp.float32
     )
@@ -111,7 +118,7 @@
 def solution(mesh):
     placed = (P("joint", "frame", None), P(), P("frame", None), P("joint", "frame", None))
     return jax.shard_map(
-        per_device,
+        per_device_body,
         mesh=mesh,
         in_specs=placed,
         out_specs=(P("joint", "frame", None), P("joint", "frame", None), P("frame", None), P()),

time: 319 us -> 346 us (1.085)
  waiting for transfers between devices: 113 us -> 160 us
  blocking collectives: 134 us -> 108 us
  starting transfers between devices: 7.13 us -> 14.6 us
    ppermute x0 -> x3, waiting for transfers between devices: none -> 38.9 us  [per_device_body(): other = lax.ppermute(weight_grad, 'joint', pairs)]
    all_gather x1 -> x0, blocking collectives: 25.1 us -> none  [per_device(): lax.all_gather(joint_part, 'joint', axis=1, tiled=True).astype(jnp.float32)]
    reduce_scatter x1, waiting for transfers between devices: 84.1 us -> 92.8 us  [per_device_body(): lax.psum_scatter((product * grad_scale).astype(jnp.bfloat16), 'frame', sc...]
    ppermute x0 -> x3, starting transfers between devices: none -> 8.28 us  [per_device_body(): other = lax.ppermute(weight_grad, 'joint', pairs)]
  transfers between devices with their start and end apart: 4 -> 6, of which waited for: 2 -> 3; matrix products, arithmetic and copies ran while one was open for 5% -> 4% of each run, Pallas kernels for 0% -> 0%
where the time goes in v7:
time: 346 us; the launch traced here: 342 us
  waiting for transfers between devices  160 us (46%)
  blocking collectives  108 us (31%)
  matrix products  28.2 us (8%)
  starting transfers between devices  14.6 us (4%)
  between operations  14.4 us (4%)
  local copies, waits for them, and re-layouts  11.2 us (3%)
  other arithmetic  6.03 us (2%)
    reduce_scatter x1, waiting for transfers between devices, per_device_body(): lax.psum_scatter((product * grad_scale).astype(jnp.bfloat16), 'frame', sc...  92.8 us
    psum x1, blocking collectives, per_device_body(): gain_grad = lax.psum(gain_part, ('joint', 'frame'))  72.1 us
    ppermute x3, waiting for transfers between devices, per_device_body(): other = lax.ppermute(weight_grad, 'joint', pairs)  38.9 us
    all_to_all x1, blocking collectives, per_device_body(): packed = lax.all_to_all(packed, 'joint', 1, 0, tiled=True)  35.6 us
    all_gather x1, waiting for transfers between devices, per_device_body(): whole = lax.all_gather(qkv_weight, 'frame', axis=0, tiled=True)  27.9 us
    ppermute x3, starting transfers between devices, per_device_body(): other = lax.ppermute(weight_grad, 'joint', pairs)  8.28 us
    dot_general x1, matrix products, per_device_body(): lax.dot_general(qkv_grad, whole, (((1,), (1,)), ((), ())), preferred_elem...  7.44 us
  transfers between devices with their start and end apart: 6, of which 3 were waited for; matrix products, arithmetic and copies ran while one was open for 4% of the time, Pallas kernels for 0%

profile of v7, /device:TPU:2, one launch (start us, length us, event | category | flops | bytes accessed | tf_op | source)
XLA Modules:
  0.0 342.3 jit_solution(16270294034885398776)
XLA Ops:
  7.2 0.0 all-gather.2.cloned.1.call-start
  7.2 0.7 all-gather.2.cloned.1.call-update
  7.9 0.0 reduce-scatter.2.cloned.1.call-start
  8.0 1.2 copy.77
  9.2 0.2 copy.76
  9.4 0.1 pad_maximum_fusion
  9.4 35.6 %all_to_all.36 = bf16[8,24,2560]{2,0,1:T(8,128)(2,1)S(1)} all-to-all(bf16[8,24,2560]{2,0,1:T(8,128)(2,1)S(1)} %pad_maximum_fusion), channel_id=1, replica_groups=mesh['joint'=8,'frame'=32] {'joint'}, dimensions={1} | all-to-all | bytes 1966080 | tf_op jit(solution)/shard_map/all_to_all | solution.py:63
  45.0 0.1 copy.149
  45.1 0.2 multiply_reduce_fusion.2
  45.3 0.1 rsqrt.12
  45.4 0.1 slice_convert_fusion
  45.5 0.0 copy-start.10
  45.6 0.1 bitcast_multiply_fusion
  45.7 27.9 %all-gather.2.cloned.1.call-done = bf16[1536,3072]{1,0:T(8,128)(2,1)} async-done(((bf16[48,3072]{1,0:T(8,128)(2,1)}), bf16[1536,3072]{1,0:T(8,128)(2,1)}) %all-gather.2.cloned.1.call-update) | async-done | bytes 9437200 | tf_op jit(solution)/shard_map/all_gather | solution.py:60
  73.6 5.7 %fusion.3 = bf16[24,8,24,128]{3,1,2,0:T(8,128)(2,1)S(1)} fusion(bf16[1536,3072]{1,0:T(8,128)(2,1)} %all-gather.2.cloned.1.call-done, f32[192,1536]{1,0:T(8,128)S(1)} %bitcast_multiply_fusion, f32[1536]{0:T(1024)S(1)} %copy-done.10), kind=kOutput, calls=%fused_computation.7 | convolution fusion | flops 1813118976 | bytes 11802624 | tf_op jit(solution)/shard_map/dot_general | solution.py:71
  79.3 0.0 copy-done
  79.4 0.2 copy.109
  79.6 1.1 fusion.28
  80.7 0.3 fusion.12
  81.0 2.4 fusion.29
  83.4 2.7 fusion.10
  86.1 2.4 fusion.8
  88.5 0.0 copy-done.3
  88.5 0.1 fusion.27
  88.6 0.9 copy.91
  89.6 2.1 convert_reduce_fusion
  91.7 0.0 copy-start.5
  91.7 0.3 copy.93
  92.0 0.9 copy.87
  92.9 2.1 convert_reduce_fusion.1
  95.0 0.3 copy.90
  95.3 0.3 copy.86
  95.6 0.1 bitcast_dynamic-update-slice_fusion.2
  95.6 0.1 bitcast_dynamic-update-slice_fusion.1
  95.7 0.1 bitcast_dynamic-update-slice_fusion
  95.8 1.0 copy-done.9
  96.8 0.4 copy-done.1
  97.2 5.1 %multiply_convert_fusion = bf16[1536,3072]{1,0:T(8,128)(2,1)} fusion(bf16[192,3072]{1,0:T(8,128)(2,1)S(1)} %bitcast_dynamic-update-slice_fusion, f32[192,1536]{1,0:T(8,128)S(1)} %copy-done.1, f32[1536]{0:T(1024)S(1)} %copy-done.10), kind=kOutput, calls=%fused_computation.2 | convolution fusion | flops 1821966336 | bytes 11802624 | tf_op jit(solution)/shard_map/dot_general | solution.py:87
  102.3 0.0 reduce-scatter.2.cloned.1.call-update
  102.3 0.3 fusion.9
  102.6 0.3 copy.102
  102.9 0.1 reshape.73
  103.0 0.9 copy-done.2
  103.9 7.4 %multiply_reduce_fusion = (f32[1536]{0:T(1024)S(1)}, f32[192]{0:T(256)S(1)}, f32[192,1536]{1,0:T(8,128)S(1)}) fusion(f32[192,1536]{1,0:T(8,128)S(1)} %copy-done.2, f32[1536]{0:T(1024)S(1)} %copy-done.10, bf16[192,3072]{1,0:T(8,128)(2,1)} %copy-done.9, bf16[1536,3072]{1,0:T(8,128)(2,1)} %all-gather.2.cloned.1.call-done), kind=kOutput, calls=%fused_computation.20 | convolution fusion | flops 1813412096 | bytes 12989184 | tf_op jit(solution)/shard_map/dot_general | solution.py:101
  111.4 0.3 multiply_convert_fusion.1
  111.7 0.5 copy.95
  112.2 92.8 %reduce-scatter.2.cloned.1.call-done = bf16[48,3072]{1,0:T(8,128)(2,1)} async-done(((bf16[1536,3072]{1,0:T(8,128)(2,1)}), bf16[48,3072]{1,0:T(8,128)(2,1)}) %reduce-scatter.2.cloned.1.call-update) | async-done | bytes 294928 | tf_op jit(solution)/shard_map/reduce_scatter | solution.py:90
  204.9 1.6 collective-permute-start
  206.5 1.7 maximum_bitcast_fusion
  208.2 6.2 %all-to-all-start.1 = ((bf16[64,3,2560]{2,1,0:T(4,128)(2,1)}), bf16[64,3,2560]{2,1,0:T(4,128)(2,1)S(1)}, u32[]{:S(2)}, u32[]{:S(2)}) async-start(bf16[64,3,2560]{2,1,0:T(4,128)(2,1)} %maximum_bitcast_fusion), calls=%async_computation.1 | async-start | bytes 2621440 | tf_op jit(solution)/shard_map/all_to_all | solution.py:112
  214.4 0.0 collective-permute-done
  214.4 0.1 add_convert_fusion.2
  214.5 3.0 collective-permute-start.1
  217.5 38.9 %collective-permute-done.1 = bf16[48,3072]{1,0:T(8,128)(2,1)S(1)} collective-permute-done((bf16[48,3072]{1,0:T(8,128)(2,1)S(1)}, bf16[48,3072]{1,0:T(8,128)(2,1)S(1)}, u32[]{:S(2)}, u32[]{:S(2)}) %collective-permute-start.1) | collective-permute-done | bytes 294944 | tf_op jit(solution)/shard_map/ppermute | solution.py:97
  256.4 0.1 add_convert_fusion.1
  256.5 3.7 %collective-permute-start.2 = (bf16[48,3072]{1,0:T(8,128)(2,1)S(1)}, bf16[48,3072]{1,0:T(8,128)(2,1)S(1)}, u32[]{:S(2)}, u32[]{:S(2)}) collective-permute-start(bf16[48,3072]{1,0:T(8,128)(2,1)S(1)} %add_convert_fusion.1), channel_id=1, source_target_pairs={{0,128},{32,160},{64,192},{96,224},{128,0},{160,32},{192,64},{224,... | collective-permute-start | bytes 884744 | tf_op jit(solution)/shard_map/ppermute | solution.py:97
  260.2 72.1 %psum.7 = f32[1536]{0:T(1024)} all-reduce(f32[1536]{0:T(1024)S(1)} %broadcast_multiply_fusion), channel_id=1, replica_groups=mesh['joint'=8,'frame'=32] {'joint','frame'}, use_global_device_ids=true, to_apply=%region_9.0 | all-reduce | flops 1536 | bytes 12288 | tf_op jit(solution)/shard_map/psum | solution.py:105
  332.3 0.0 all-to-all-done.1
  332.3 0.2 copy.148
  332.5 0.1 copy.97
  332.7 1.0 copy.99
  333.7 1.0 copy.98
  334.6 0.0 collective-permute-done.2
  334.6 0.9 fusion.20
  (20 shorter events, 0.1 us)
Async XLA Ops:
  7.2 2.0 copy-start.4
  7.2 66.5 %all-gather.2.cloned.1.call-start = ((), (), s32[]{:S(2)}) async-start(), calls=%async_computation.3 | async-start | bytes 9732096 | tf_op jit(solution)/shard_map/all_gather | solution.py:60
  7.9 197.0 %reduce-scatter.2.cloned.1.call-start = ((), (), s32[]{:S(2)}) async-start(), calls=%async_computation.4 | async-start | bytes 9732096 | tf_op jit(solution)/shard_map/reduce_scatter | solution.py:90
  45.5 28.1 %copy-start.10 = (f32[1536]{0:T(1024)S(1)}, f32[1536]{0:T(1024)}, u32[]{:S(2)}) copy-start(f32[1536]{0:T(1024)} %param.5) | copy-start | bytes 18436
  45.7 33.6 %copy-start = (f32[192,1536]{1,0:T(8,128)}, f32[192,1536]{1,0:T(8,128)S(1)}, u32[]{:S(2)}) copy-start(f32[192,1536]{1,0:T(8,128)S(1)} %bitcast_multiply_fusion) | copy-start | bytes 3538948
  86.1 2.4 copy-start.3
  89.6 2.4 copy-start.7
  91.7 1.2 copy-start.5
  92.9 2.4 copy-start.6
  95.6 1.7 copy-start.1
  95.7 1.0 copy-start.9
  102.6 1.3 copy-start.2
  204.9 9.5 %collective-permute-start = (bf16[48,3072]{1,0:T(8,128)(2,1)}, bf16[48,3072]{1,0:T(8,128)(2,1)S(1)}, u32[]{:S(2)}, u32[]{:S(2)}) collective-permute-start(bf16[48,3072]{1,0:T(8,128)(2,1)} %reduce-scatter.2.cloned.1.call-done), channel_id=1, source_target_pairs={{0,32},{32,0},{64,96},{96,64},{128,160},{160,128},{192,224},{224,1... | collective-permute-start | bytes 884744 | tf_op jit(solution)/shard_map/ppermute | solution.py:97
  208.2 6.3 %copy-start.8 = (bf16[48,3072]{1,0:T(8,128)(2,1)S(1)}, bf16[48,3072]{1,0:T(8,128)(2,1)}, u32[]{:S(2)}) copy-start(bf16[48,3072]{1,0:T(8,128)(2,1)} %reduce-scatter.2.cloned.1.call-done) | copy-start | bytes 884740
  208.2 124.1 %all-to-all-start.1 = ((bf16[64,3,2560]{2,1,0:T(4,128)(2,1)}), bf16[64,3,2560]{2,1,0:T(4,128)(2,1)S(1)}, u32[]{:S(2)}, u32[]{:S(2)}) async-start(bf16[64,3,2560]{2,1,0:T(4,128)(2,1)} %maximum_bitcast_fusion), calls=%async_computation.1 | async-start | bytes 2621440 | tf_op jit(solution)/shard_map/all_to_all | solution.py:112
  214.5 41.9 %collective-permute-start.1 = (bf16[48,3072]{1,0:T(8,128)(2,1)S(1)}, bf16[48,3072]{1,0:T(8,128)(2,1)S(1)}, u32[]{:S(2)}, u32[]{:S(2)}) collective-permute-start(bf16[48,3072]{1,0:T(8,128)(2,1)S(1)} %add_convert_fusion.2), channel_id=1, source_target_pairs={{0,64},{32,96},{64,0},{96,32},{128,192},{160,224},{192,128},{224,1... | collective-permute-start | bytes 884744 | tf_op jit(solution)/shard_map/ppermute | solution.py:97
  256.5 78.1 %collective-permute-start.2 = (bf16[48,3072]{1,0:T(8,128)(2,1)S(1)}, bf16[48,3072]{1,0:T(8,128)(2,1)S(1)}, u32[]{:S(2)}, u32[]{:S(2)}) collective-permute-start(bf16[48,3072]{1,0:T(8,128)(2,1)S(1)} %add_convert_fusion.1), channel_id=1, source_target_pairs={{0,128},{32,160},{64,192},{96,224},{128,0},{160,32},{192,64},{224,... | collective-permute-start | bytes 884744 | tf_op jit(solution)/shard_map/ppermute | solution.py:97
Sparse Core Ops, SparseCore 0:
  10.5 63.0 all-gather.1
  102.5 102.4 reduce-scatter.1

commit v8 on v1

--- a/solution.py
+++ b/solution.py
@@ -4,6 +4,7 @@
 import jax.numpy as jnp
 from jax import lax
 from jax.sharding import PartitionSpec as P
+
 
 HEADS = 8
 HDIM = 128
@@ -45,7 +46,7 @@
     return attended, query_grad, key_grad, value_grad
 
 
-def per_device(tokens, norm_gain, qkv_weight, out_grad):
+def per_device_body(tokens, norm_gain, qkv_weight, out_grad):
     joint_rows, frame_rows, width = tokens.shape
     inner = out_grad.shape[2]
     joint_count = lax.axis_size("joint")
@@ -89,8 +90,8 @@
     frame_sum = lax.psum_scatter(
         (product * grad_scale).astype(jnp.bfloat16), "frame", scatter_dimension=0, tiled=True
     )
-    joint_part = lax.psum_scatter(frame_sum, "joint", scatter_dimension=1, tiled=True)
-    weight_grad = lax.all_gather(joint_part, "joint", axis=1, tiled=True).astype(jnp.float32)
+    gathered = lax.all_gather(frame_sum, "joint", axis=0)
+    weight_grad = jnp.sum(gathered.astype(jnp.float32), axis=0)
     normed_grad = lax.dot_general(
         qkv_grad, whole, (((1,), (1,)), ((), ())), preferred_element_type=jnp.float32
     )
@@ -111,7 +112,7 @@
 def solution(mesh):
     placed = (P("joint", "frame", None), P(), P("frame", None), P("joint", "frame", None))
     return jax.shard_map(
-        per_device,
+        per_device_body,
         mesh=mesh,
         in_specs=placed,
         out_specs=(P("joint", "frame", None), P("joint", "frame", None), P("frame", None), P()),

time: 319 us -> 326 us (1.022)
  waiting for transfers between devices: 113 us -> 131 us
  blocking collectives: 134 us -> 123 us
    all_gather x1 -> x0, blocking collectives: 25.1 us -> none  [per_device(): lax.all_gather(joint_part, 'joint', axis=1, tiled=True).astype(jnp.float32)]
    reduce_scatter x1, waiting for transfers between devices: 84.1 us -> 102 us  [per_device_body(): lax.psum_scatter((product * grad_scale).astype(jnp.bfloat16), 'frame', sc...]
    psum x1, blocking collectives: 73.7 us -> 87.7 us  [per_device_body(): gain_grad = lax.psum(gain_part, ('joint', 'frame'))]
    unnamed x29 -> x27, local copies, waits for them, and re-layouts: 9.18 us -> 6.03 us
    all_gather x1 -> x2, waiting for transfers between devices: 27.9 us -> 27.9 us  [the longest x1 27.9 us: per_device_body(): whole = lax.all_gather(qkv_weight, 'frame', axis=0, tiled=True)]
where the time goes in v8:
time: 326 us; the launch traced here: 323 us
  waiting for transfers between devices  131 us (40%)
  blocking collectives  123 us (38%)
  matrix products  28.2 us (9%)
  between operations  14 us (4%)
  local copies, waits for them, and re-layouts  11.2 us (3%)
  other arithmetic  7.88 us (2%)
  starting transfers between devices  7.33 us (2%)
    reduce_scatter x1, waiting for transfers between devices, per_device_body(): lax.psum_scatter((product * grad_scale).astype(jnp.bfloat16), 'frame', sc...  102 us
    psum x1, blocking collectives, per_device_body(): gain_grad = lax.psum(gain_part, ('joint', 'frame'))  87.7 us
    all_to_all x1, blocking collectives, per_device_body(): packed = lax.all_to_all(packed, 'joint', 1, 0, tiled=True)  35.6 us
    all_gather x1, waiting for transfers between devices, per_device_body(): whole = lax.all_gather(qkv_weight, 'frame', axis=0, tiled=True)  27.9 us
    dot_general x1, matrix products, per_device_body(): lax.dot_general(qkv_grad, whole, (((1,), (1,)), ((), ())), preferred_elem...  7.45 us
    all_to_all x1, starting transfers between devices, per_device_body(): back = lax.all_to_all(back, 'joint', 0, 1, tiled=True)  7.03 us
  transfers between devices with their start and end apart: 4, of which 2 were waited for; matrix products, arithmetic and copies ran while one was open for 5% of the time, Pallas kernels for 0%

profile of v8, /device:TPU:2, one launch (start us, length us, event | category | flops | bytes accessed | tf_op | source)
XLA Modules:
  0.0 322.9 jit_solution(845233717993030430)
XLA Ops:
  7.2 0.0 copy-start.4
  7.2 0.0 all-gather.4.cloned.1.call-start
  7.2 0.7 all-gather.4.cloned.1.call-update
  7.9 0.0 reduce-scatter.2.cloned.1.call-start
  8.0 1.2 copy.77
  9.2 0.0 copy-done.4
  9.2 0.2 copy.76
  9.4 0.1 pad_maximum_fusion
  9.4 35.6 %all_to_all.36 = bf16[8,24,2560]{2,0,1:T(8,128)(2,1)S(1)} all-to-all(bf16[8,24,2560]{2,0,1:T(8,128)(2,1)S(1)} %pad_maximum_fusion), channel_id=1, replica_groups=mesh['joint'=8,'frame'=32] {'joint'}, dimensions={1} | all-to-all | bytes 1966080 | tf_op jit(solution)/shard_map/all_to_all | solution.py:63
  45.0 0.1 copy.149
  45.1 0.2 multiply_reduce_fusion.2
  45.3 0.1 rsqrt.12
  45.4 0.1 slice_convert_fusion
  45.5 0.0 copy-start.9
  45.6 0.1 bitcast_multiply_fusion
  45.7 0.0 copy-start
  45.7 27.9 %all-gather.4.cloned.1.call-done = bf16[1536,3072]{1,0:T(8,128)(2,1)} async-done(((bf16[48,3072]{1,0:T(8,128)(2,1)}), bf16[1536,3072]{1,0:T(8,128)(2,1)}) %all-gather.4.cloned.1.call-update) | async-done | bytes 9437200 | tf_op jit(solution)/shard_map/all_gather | solution.py:60
  73.6 5.7 %fusion.3 = bf16[24,8,24,128]{3,1,2,0:T(8,128)(2,1)S(1)} fusion(bf16[1536,3072]{1,0:T(8,128)(2,1)} %all-gather.4.cloned.1.call-done, f32[192,1536]{1,0:T(8,128)S(1)} %bitcast_multiply_fusion, f32[1536]{0:T(1024)S(1)} %copy-done.9), kind=kOutput, calls=%fused_computation.8 | convolution fusion | flops 1813118976 | bytes 11802624 | tf_op jit(solution)/shard_map/dot_general | solution.py:71
  79.3 0.0 copy-done
  79.4 0.2 copy.109
  79.6 1.1 fusion.27
  80.7 0.3 fusion.12
  81.0 2.4 fusion.28
  83.4 2.7 fusion.10
  86.1 2.4 fusion.8
  88.5 0.0 copy-done.3
  88.5 0.1 fusion.26
  88.6 0.9 copy.91
  89.6 2.1 convert_reduce_fusion.1
  91.7 0.0 copy-start.5
  91.7 0.3 copy.93
  92.0 0.9 copy.87
  92.9 0.0 copy-done.5
  92.9 2.1 convert_reduce_fusion.2
  95.0 0.3 copy.90
  95.3 0.0 copy-done.6
  95.3 0.3 copy.86
  95.6 0.0 copy-start.1
  95.6 0.1 bitcast_dynamic-update-slice_fusion.2
  95.6 0.1 bitcast_dynamic-update-slice_fusion.1
  95.7 0.1 bitcast_dynamic-update-slice_fusion
  95.8 1.0 copy-done.8
  96.8 0.4 copy-done.1
  97.2 5.1 %multiply_convert_fusion = bf16[1536,3072]{1,0:T(8,128)(2,1)} fusion(bf16[192,3072]{1,0:T(8,128)(2,1)S(1)} %bitcast_dynamic-update-slice_fusion, f32[192,1536]{1,0:T(8,128)S(1)} %copy-done.1, f32[1536]{0:T(1024)S(1)} %copy-done.9), kind=kOutput, calls=%fused_computation.2 | convolution fusion | flops 1821966336 | bytes 11802624 | tf_op jit(solution)/shard_map/dot_general | solution.py:87
  102.3 0.0 reduce-scatter.2.cloned.1.call-update
  102.3 0.2 all-gather.6.cloned.1.call-start
  102.6 102.4 %reduce-scatter.2.cloned.1.call-done = bf16[48,3072]{1,0:T(8,128)(2,1)} async-done(((bf16[1536,3072]{1,0:T(8,128)(2,1)}), bf16[48,3072]{1,0:T(8,128)(2,1)}) %reduce-scatter.2.cloned.1.call-update) | async-done | bytes 294928 | tf_op jit(solution)/shard_map/reduce_scatter | solution.py:90
  204.9 0.0 all-gather.6.cloned.1.call-update
  205.0 0.3 fusion.9
  205.3 0.3 copy.102
  205.5 0.1 reshape.75
  205.7 0.9 copy-done.2
  206.5 7.4 %multiply_reduce_fusion = (f32[1536]{0:T(1024)S(1)}, f32[192]{0:T(256)S(1)}, f32[192,1536]{1,0:T(8,128)S(1)}) fusion(f32[192,1536]{1,0:T(8,128)S(1)} %copy-done.2, f32[1536]{0:T(1024)S(1)} %copy-done.9, bf16[192,3072]{1,0:T(8,128)(2,1)} %copy-done.8, bf16[1536,3072]{1,0:T(8,128)(2,1)} %all-gather.4.cloned.1.call-done), kind=kOutput, calls=%fused_computation.21 | convolution fusion | flops 1813412096 | bytes 12989184 | tf_op jit(solution)/shard_map/dot_general | solution.py:95
  214.0 0.3 multiply_convert_fusion.1
  214.3 0.5 copy.95
  214.8 1.7 maximum_bitcast_fusion
  216.5 7.0 %all-to-all-start.1 = ((bf16[64,3,2560]{2,1,0:T(4,128)(2,1)}), bf16[64,3,2560]{2,1,0:T(4,128)(2,1)S(1)}, u32[]{:S(2)}, u32[]{:S(2)}) async-start(bf16[64,3,2560]{2,1,0:T(4,128)(2,1)} %maximum_bitcast_fusion), calls=%async_computation.1 | async-start | bytes 2621440 | tf_op jit(solution)/shard_map/all_to_all | solution.py:106
  223.5 87.7 %psum.7 = f32[1536]{0:T(1024)} all-reduce(f32[1536]{0:T(1024)S(1)} %broadcast_multiply_fusion), channel_id=1, replica_groups=mesh['joint'=8,'frame'=32] {'joint','frame'}, use_global_device_ids=true, to_apply=%region_10.0 | all-reduce | flops 1536 | bytes 12288 | tf_op jit(solution)/shard_map/psum | solution.py:99
  311.2 0.0 all-to-all-done.1
  311.2 0.2 copy.148
  311.4 0.1 copy.97
  311.6 1.0 copy.99
  312.5 1.0 copy.98
  313.5 2.9 convert_reduce_fusion
  (13 shorter events, 0.1 us)
Async XLA Ops:
  7.2 2.0 copy-start.4
  7.2 66.5 %all-gather.4.cloned.1.call-start = ((), (), s32[]{:S(2)}) async-start(), calls=%async_computation.3 | async-start | bytes 9732096 | tf_op jit(solution)/shard_map/all_gather | solution.py:60
  7.9 197.0 %reduce-scatter.2.cloned.1.call-start = ((), (), s32[]{:S(2)}) async-start(), calls=%async_computation.4 | async-start | bytes 9732096 | tf_op jit(solution)/shard_map/reduce_scatter | solution.py:90
  45.5 28.1 %copy-start.9 = (f32[1536]{0:T(1024)S(1)}, f32[1536]{0:T(1024)}, u32[]{:S(2)}) copy-start(f32[1536]{0:T(1024)} %param.5) | copy-start | bytes 18436
  45.7 33.6 %copy-start = (f32[192,1536]{1,0:T(8,128)}, f32[192,1536]{1,0:T(8,128)S(1)}, u32[]{:S(2)}) copy-start(f32[192,1536]{1,0:T(8,128)S(1)} %bitcast_multiply_fusion) | copy-start | bytes 3538948
  86.1 2.4 copy-start.3
  89.6 2.4 copy-start.7
  91.7 1.2 copy-start.5
  92.9 2.4 copy-start.6
  95.6 1.7 copy-start.1
  95.7 1.0 copy-start.8
  102.3 211.2 %all-gather.6.cloned.1.call-start = ((), (), s32[]{:S(2)}) async-start(), calls=%async_computation.5 | async-start | bytes 2654208 | tf_op jit(solution)/shard_map/all_gather | solution.py:93
  205.3 1.3 copy-start.2
  216.5 94.7 %all-to-all-start.1 = ((bf16[64,3,2560]{2,1,0:T(4,128)(2,1)}), bf16[64,3,2560]{2,1,0:T(4,128)(2,1)S(1)}, u32[]{:S(2)}, u32[]{:S(2)}) async-start(bf16[64,3,2560]{2,1,0:T(4,128)(2,1)} %maximum_bitcast_fusion), calls=%async_computation.1 | async-start | bytes 2621440 | tf_op jit(solution)/shard_map/all_to_all | solution.py:106
Sparse Core Ops, SparseCore 0:
  10.5 63.0 all-gather.3
  102.5 102.4 reduce-scatter.1
  206.7 66.6 all-gather.5
